TPU v7x, 1024 devices: a whole 4x4x32 slice. The times are simulated.
1024 devices in a mesh: ctx: 128 (over z, y), head: 8 (over x, core).
Axes of the slice: x: 4, y: 4, z: 32, core: 2. Of those that a mesh axis runs over, the one named last changes fastest.
Arguments:
- queries: bfloat16 [32768, 4096], P('ctx', 'head'), may hold values from -6 to 6
- key_rows: bfloat16 [32768, 4096], P('ctx', 'head'), may hold values from -1.5 to 1.5
- value_rows: bfloat16 [32768, 4096], P('ctx', 'head'), may hold values from -6 to 6
- carry_state: float32 [32, 128, 128], P('head'), may hold values from -96 to 96
- decay_rate: float32 [32], P('head'), as said below
- norm_gain: float32 [4096], P('head'), may hold values from 0.5 to 1.5
- order: int32 [128, 256], P('ctx'), may hold values from 0 to 255, each once within a row
- doc_lengths: int32 [256], replicated, may hold values from 1 to 2048, 32768 in all
Outputs:
- mixed: bfloat16 [32768, 4096], P('ctx', 'head')
Inputs may be any that keep to these rules, and one draw needn't show every extreme that they name: `order`: each row is a permutation of 0..255. `doc_lengths`: they sum to 32768; the longest is exactly 2048. `decay_rate`: positive rates.
All inputs are finite; a program needn't handle non-finite values.
Results may differ from a plain program's by a relative error of at most 0.001.
Values may be sent and summed in bfloat16 or wider, within the bound.
No kernel may reach another device: no remote copies, remote signals or barrier semaphores. Data moves between devices by JAX's collectives and lax.ppermute only.
A program may use at most 128 MiB of HBM per device.

v0:
```python
import jax
import jax.numpy as jnp
from jax import lax
from jax.sharding import PartitionSpec as P


def from_behind(value, axis, steps):
    count = lax.axis_size(axis)
    pairs = [(source, (source + steps) % count) for source in range(count)]
    return lax.ppermute(value, axis, pairs)


def entering(value, axis, combine, identity):
    peers, position = (lax.axis_size(axis), lax.axis_index(axis))
    everything = jax.tree.map(lambda part: lax.all_gather(part, axis), value)
    start = jax.tree.map(
        lambda part, zero: jnp.broadcast_to(jnp.asarray(zero, part.dtype), part.shape),
        value,
        identity,
    )

    def lap(k, before):
        reached = k < position
        new = combine(before, jax.tree.map(lambda part: part[k], everything))
        return jax.tree.map(lambda a, b: jnp.where(reached, a, b), new, before)

    return lax.fori_loop(0, peers, lap, start)


def shards(queries, key_rows, value_rows, carry_state, decay_rate, norm_gain, order, doc_lengths):
    row_count, feature_count = queries.shape
    head_count = decay_rate.shape[0]
    head_width = feature_count // head_count
    spill_count = row_count // 4
    block_size = min(512, row_count)
    highest = lax.Precision.HIGHEST
    permuted = order[0]
    kept_rows = permuted[: row_count - spill_count]
    moved_rows = permuted[row_count - spill_count :]
    outgoing = jnp.stack([queries[moved_rows], key_rows[moved_rows], value_rows[moved_rows]])
    arrived = from_behind(outgoing, "ctx", -1)
    ctx_query = jnp.concatenate([queries[kept_rows], arrived[0]], axis=0)
    ctx_key = jnp.concatenate([key_rows[kept_rows], arrived[1]], axis=0)
    ctx_value = jnp.concatenate([value_rows[kept_rows], arrived[2]], axis=0)
    device = lax.axis_index("ctx")
    offset_base = device * row_count
    doc_ends = jnp.cumsum(doc_lengths)

    def count_before(position):
        return jnp.sum((doc_ends <= position).astype(jnp.int32))

    positions = offset_base + jnp.arange(row_count, dtype=jnp.int32)
    segment = jnp.sum((doc_ends[None, :] <= positions[:, None]).astype(jnp.int32), axis=1)
    prior_device = count_before(offset_base - 1)
    offsets = jnp.arange(block_size, dtype=jnp.int32)
    distance = offsets[:, None] - offsets[None, :]
    lower = distance >= 0
    decay = jnp.exp(-decay_rate[:, None, None] * jnp.maximum(distance, 0).astype(jnp.float32)[None])
    leading = jnp.exp(-decay_rate[None, :] * (offsets + 1).astype(jnp.float32)[:, None])
    trailing = jnp.exp(
        -decay_rate[None, :] * (block_size - 1 - offsets).astype(jnp.float32)[:, None]
    )
    whole_block = jnp.exp(-decay_rate * jnp.float32(block_size))
    running = jnp.zeros((head_count, head_width, head_width), jnp.float32)
    query_block = ctx_query.reshape(block_size, head_count, head_width)
    key_block = ctx_key.reshape(block_size, head_count, head_width)
    value_block = ctx_value.reshape(block_size, head_count, head_width)
    prior = count_before(offset_base + 0 - 1)
    same_doc = (segment[:, None] == segment[None, :]) & lower
    scores = jnp.einsum("thd,shd->hts", query_block, key_block, preferred_element_type=jnp.float32)
    weights = jnp.where(same_doc[None], scores * decay, jnp.float32(0.0))
    value_f = value_block.astype(jnp.float32)
    attn = jnp.einsum("hts,shd->thd", weights, value_f, precision=highest)
    carry_on = (segment == prior).astype(jnp.float32)
    inter = jnp.einsum("thd,hde->the", query_block.astype(jnp.float32), running, precision=highest)
    attn = attn + inter * (leading * carry_on[:, None])[:, :, None]
    at_end = (segment == segment[-1]).astype(jnp.float32)
    scaled_keys = key_block.astype(jnp.float32) * (trailing * at_end[:, None])[:, :, None]
    added = jnp.einsum("shd,she->hde", scaled_keys, value_f, precision=highest)
    keep_factor = jnp.where(segment[-1] == prior, whole_block, jnp.float32(0.0))
    running = keep_factor[:, None, None] * running + added
    local_attn = attn
    reach = jnp.where(
        segment[-1] == prior_device, jnp.exp(-decay_rate * jnp.float32(row_count)), jnp.float32(0.0)
    )
    initial = carry_state * (device == 0).astype(jnp.float32)
    element = reach[:, None, None] * initial + running

    def combine(earlier, latter):
        return (earlier[0] * latter[0], latter[0][:, None, None] * earlier[1] + latter[1])

    identity = (jnp.ones_like(reach), jnp.zeros_like(element))
    incoming = entering((reach, element), "ctx", combine, identity)[1]
    incoming = incoming + initial
    device_on = (segment == prior_device).astype(jnp.float32)
    local_offsets = jnp.arange(row_count, dtype=jnp.int32)
    lead_all = (
        jnp.exp(-decay_rate[None, :] * (local_offsets + 1).astype(jnp.float32)[:, None])
        * device_on[:, None]
    )
    query_all = ctx_query.reshape(row_count, head_count, head_width).astype(jnp.float32)
    carried = jnp.einsum("thd,hde->the", query_all, incoming, precision=highest)
    local_attn = local_attn + carried * lead_all[:, :, None]
    flat = local_attn.reshape(row_count, feature_count)
    square_total = lax.psum(jnp.sum(flat * flat, axis=1), "head")
    mean_sq = square_total / jnp.float32(feature_count * lax.axis_size("head"))
    normed = (flat * lax.rsqrt(mean_sq + 1e-05)[:, None] * norm_gain[None, :]).astype(jnp.bfloat16)
    returned = from_behind(normed[row_count - spill_count :], "ctx", 1)
    result = jnp.zeros_like(queries).at[kept_rows].set(normed[: row_count - spill_count])
    return result.at[moved_rows].set(returned)


def solution(mesh):
    return jax.shard_map(
        shards,
        mesh=mesh,
        in_specs=(
            P("ctx", "head"),
            P("ctx", "head"),
            P("ctx", "head"),
            P("head", None, None),
            P("head"),
            P("head"),
            P("ctx", None),
            P(),
        ),
        out_specs=P("ctx", "head"),
        check_vma=False,
    )
```

profile of v0, /device:TPU:1, one launch (start us, length us, event | category | flops | bytes accessed | tf_op | source)
XLA Modules:
  0.0 595.7 jit_solution(1946033936578659553)
XLA Ops:
  8.0 1.7 gather_fusion.1
  10.4 1.7 gather_fusion.3
  12.1 21.7 %collective-permute-start = (bf16[3,64,512]{2,1,0:T(8,128)(2,1)S(1)}, bf16[3,64,512]{2,1,0:T(8,128)(2,1)S(1)}, u32[]{:S(2)}, u32[]{:S(2)}) collective-permute-start(bf16[3,64,512]{2,1,0:T(8,128)(2,1)S(1)} %pad_maximum_fusion.1), channel_id=1, source_target_pairs={{0,1016},{8,0},{16,8},{24,16},{32,24},{40,32},{48,40},{56,48},{64,... | collective-permute-start | bytes 589832 | tf_op jit(solution)/shard_map/ppermute | solution.py:10
  36.6 1.3 compare_convert_fusion.1
  40.3 2.0 gather_fusion
  43.5 2.4 fusion.6
  46.0 2.0 gather_fusion.4
  48.0 1.4 dynamic-slice
  50.3 222.2 %all-reduce = f32[512]{0:T(512)S(1)} all-reduce(f32[512]{0:T(512)S(1)} %dynamic-update-slice), channel_id=2, replica_groups=mesh['ctx'=128,'head'=8] {'ctx'}, use_global_device_ids=true, to_apply=%add | all-reduce | flops 512 | bytes 4096
  273.6 148.4 %all-gather.4.cloned.1.call-done = f32[512,128,128]{2,1,0:T(8,128)} async-done(((f32[4,128,128]{2,1,0:T(8,128)}), f32[512,128,128]{2,1,0:T(8,128)}) %all-gather.4.cloned.1.call-update) | async-done | bytes 33554448 | tf_op jit(solution)/shard_map/all_gather | solution.py:15
  422.0 140.0 %while.14 = (s32[]{:T(128)}, f32[4,128,128]{2,1,0:T(8,128)S(1)}, s32[]{:T(128)}, f32[128,4]{1,0:T(8,128)S(1)}, f32[128,4,128,128]{3,2,1,0:T(8,128)}, /*index=5*/s32[]{:T(128)}, s32[]{:T(128)}) while((s32[]{:T(128)}, f32[4,128,128]{2,1,0:T(8,128)S(1)}, s32[]{:T(128)}, f32[128,4]{1,0:T(8,128)S(1)}, f32[128,4,128,128]{3,2,1,0:T(8,128)}, ...), condition=%wide.region_5.6_spmd.clone, body=%wide.region_4.5_spmd.clone.sunk | while | flops 262148 | bytes 786585 | solution.py:27
  425.3 1.1 fusion.33
  426.4 1.1 fusion.33
  429.6 1.1 fusion.33
  430.7 1.1 fusion.33
  431.8 1.1 fusion.33
  435.1 1.1 fusion.33
  436.2 1.1 fusion.33
  437.3 1.1 fusion.33
  440.6 1.1 fusion.33
  441.7 1.1 fusion.33
  442.8 1.1 fusion.33
  446.0 1.1 fusion.33
  447.1 1.1 fusion.33
  450.4 1.1 fusion.33
  451.5 1.1 fusion.33
  452.6 1.1 fusion.33
  455.9 1.1 fusion.33
  457.0 1.1 fusion.33
  458.1 1.1 fusion.33
  461.3 1.1 fusion.33
  462.4 1.1 fusion.33
  463.5 1.1 fusion.33
  466.8 1.1 fusion.33
  467.9 1.1 fusion.33
  471.2 1.1 fusion.33
  472.3 1.1 fusion.33
  473.4 1.1 fusion.33
  476.7 1.1 fusion.33
  477.8 1.1 fusion.33
  478.8 1.1 fusion.33
  482.1 1.1 fusion.33
  561.9 1.4 fusion.5
  564.3 12.9 %psum.7 = f32[256]{0:T(256)S(1)} all-reduce(f32[256]{0:T(256)S(1)} %get-tuple-element.140), channel_id=1, replica_groups=mesh['ctx'=128,'head'=8] {'head'}, use_global_device_ids=true, to_apply=%region_7.8 | all-reduce | flops 256 | bytes 2048 | tf_op jit(solution)/shard_map/psum | solution.py:105
  578.0 1.9 collective-permute-start.1
  580.0 2.0 scatter_custom_fusion
  581.9 4.4 collective-permute-done.1
  586.4 2.5 scatter_fusion
  (269 shorter events, 113.4 us)
Async XLA Ops:
  6.5 3.2 copy-start
  6.5 415.4 %all-gather.4.cloned.1.call-start = ((), (), s32[]{:S(2)}) async-start(), calls=%async_computation | async-start | bytes 33816576 | tf_op jit(solution)/shard_map/all_gather | solution.py:15
  12.1 31.1 %collective-permute-start = (bf16[3,64,512]{2,1,0:T(8,128)(2,1)S(1)}, bf16[3,64,512]{2,1,0:T(8,128)(2,1)S(1)}, u32[]{:S(2)}, u32[]{:S(2)}) collective-permute-start(bf16[3,64,512]{2,1,0:T(8,128)(2,1)S(1)} %pad_maximum_fusion.1), channel_id=1, source_target_pairs={{0,1016},{8,0},{16,8},{24,16},{32,24},{40,32},{48,40},{56,48},{64,... | collective-permute-start | bytes 589832 | tf_op jit(solution)/shard_map/ppermute | solution.py:10
  578.0 8.3 %collective-permute-start.1 = (bf16[64,512]{1,0:T(8,128)(2,1)S(1)}, bf16[64,512]{1,0:T(8,128)(2,1)S(1)}, u32[]{:S(2)}, u32[]{:S(2)}) collective-permute-start(bf16[64,512]{1,0:T(8,128)(2,1)S(1)} %slice.67), channel_id=1, source_target_pairs={{0,8},{8,16},{16,24},{24,32},{32,40},{40,48},{48,56},{56,64},{64,7... | collective-permute-start | bytes 196616 | tf_op jit(solution)/shard_map/ppermute | solution.py:10
Sparse Core Ops, SparseCore 0:
  46.1 375.8 all-gather.3
where the time goes:
time: 600 us; the launch traced here: 596 us
  blocking collectives  235 us (39%)
  waiting for transfers between devices  153 us (26%)
  other arithmetic  141 us (24%)
  starting transfers between devices  23.6 us (4%)
  local copies, waits for them, and re-layouts  18 us (3%)
  between operations  15.7 us (3%)
    unnamed x1, blocking collectives  222 us
    all_gather x1, waiting for transfers between devices, entering(): everything = jax.tree.map(lambda part: lax.all_gather(part, axis), value)  148 us
    select_n x128, other arithmetic, lap(): return jax.tree.map(lambda a, b: jnp.where(reached, a, b), new, before)  135 us
    ppermute x2, starting transfers between devices, from_behind(): return lax.ppermute(value, axis, pairs)  23.6 us
    psum x1, blocking collectives, shards(): square_total = lax.psum(jnp.sum(flat * flat, axis=1), 'head')  12.9 us
  transfers between devices with their start and end apart: 3, of which 2 were waited for; matrix products, arithmetic and copies ran while one was open for 2% of the time, Pallas kernels for 0%

commit v1 on v0

v1 whole, which is shorter than its diff:
```python
import jax
import jax.numpy as jnp
from jax import lax
from jax.sharding import PartitionSpec as P


def shifted(value, axis, steps, wrap_sources=()):
    count = lax.axis_size(axis)
    pairs = [(source, source + steps) for source in range(count - steps)]
    pairs += [(source, (source + steps) % count) for source in wrap_sources]
    return lax.ppermute(value, axis, pairs)


def shards(queries, key_rows, value_rows, carry_state, decay_rate, norm_gain, order, doc_lengths):
    row_count, feature_count = queries.shape
    head_count = decay_rate.shape[0]
    head_width = feature_count // head_count
    spill_count = row_count // 4
    kept_count = row_count - spill_count
    ctx_count = lax.axis_size("ctx")
    total = row_count * ctx_count
    highest = lax.Precision.HIGHEST
    device = lax.axis_index("ctx")
    rates = decay_rate.astype(jnp.float32)
    doc_ends = jnp.cumsum(doc_lengths)

    def doc_of(position):
        return jnp.sum((doc_ends[None, :] <= position[:, None]).astype(jnp.int32), axis=1)

    rows = jnp.arange(row_count, dtype=jnp.int32)
    slot_of_column = (rows + spill_count) % row_count
    window = jnp.sum(
        jnp.where(order[0][None, :] == rows[:, None], slot_of_column[None, :], 0), axis=1
    )
    position = (device * row_count - spill_count + window) % total
    segment = doc_of(position)

    def window_bounds(index):
        first = index == 0
        prior_pos = jnp.where(first, -1, index * row_count - spill_count - 1)
        end_pos = index * row_count + kept_count - 1
        prior_seg = doc_of(prior_pos)
        end_seg = doc_of(end_pos)
        span = jnp.where(first, kept_count, row_count).astype(jnp.float32)
        through = jnp.where(
            (prior_seg == end_seg)[:, None], jnp.exp(-rates[None, :] * span[:, None]), jnp.float32(0.0)
        )
        return end_seg, through

    near = (device - jnp.arange(5, dtype=jnp.int32)) % ctx_count
    end_segs, through = window_bounds(near)
    in_seg = doc_of(((device * row_count - spill_count - 1) % total)[None])[0]
    end_seg = end_segs[0]

    q = queries.reshape(row_count, head_count, head_width)
    k = key_rows.reshape(row_count, head_count, head_width)
    v = value_rows.reshape(row_count, head_count, head_width)
    q_f = q.astype(jnp.float32)
    k_f = k.astype(jnp.float32)
    v_f = v.astype(jnp.float32)

    at_end = segment == end_seg
    trailing = jnp.where(
        at_end[:, None],
        jnp.exp(-rates[None, :] * (row_count - 1 - window).astype(jnp.float32)[:, None]),
        jnp.float32(0.0),
    )
    running = jnp.einsum("shd,she->hde", k_f * trailing[:, :, None], v_f, precision=highest)
    initial = carry_state * (device == 0).astype(jnp.float32)
    element = through[0][:, None, None] * initial + running

    got = shifted(element, "ctx", 1)
    pair = through[0][:, None, None] * got + element
    got = shifted(pair, "ctx", 2)
    quad = (through[0] * through[1])[:, None, None] * got + pair
    near_quad = shifted(quad, "ctx", 1, wrap_sources=(ctx_count - 1,))
    far_quad = shifted(quad, "ctx", 5, wrap_sources=(ctx_count - 5,))
    span4 = through[1] * through[2] * through[3] * through[4]
    incoming = span4[:, None, None] * far_quad + near_quad

    distance = window[:, None] - window[None, :]
    same_doc = (segment[:, None] == segment[None, :]) & (distance >= 0)
    decay = jnp.exp(-rates[:, None, None] * jnp.maximum(distance, 0).astype(jnp.float32)[None])
    scores = jnp.einsum("thd,shd->hts", q, k, preferred_element_type=jnp.float32)
    weights = jnp.where(same_doc[None], scores * decay, jnp.float32(0.0))
    attn = jnp.einsum("hts,shd->thd", weights, v_f, precision=highest)

    lead_in = jnp.where(
        (segment == in_seg)[:, None],
        jnp.exp(-rates[None, :] * (window + 1).astype(jnp.float32)[:, None]),
        jnp.float32(0.0),
    )
    lead_init = jnp.where(
        ((segment == 0) & (device == 0))[:, None],
        jnp.exp(-rates[None, :] * (window - spill_count + 1).astype(jnp.float32)[:, None]),
        jnp.float32(0.0),
    )
    carried = jnp.einsum("thd,hde->the", q_f, incoming, precision=highest)
    started = jnp.einsum("thd,hde->the", q_f, initial, precision=highest)
    attn = attn + carried * lead_in[:, :, None] + started * lead_init[:, :, None]

    flat = attn.reshape(row_count, feature_count)
    square_total = lax.psum(jnp.sum(flat * flat, axis=1), "head")
    mean_sq = square_total / jnp.float32(feature_count * lax.axis_size("head"))
    return (flat * lax.rsqrt(mean_sq + 1e-05)[:, None] * norm_gain[None, :]).astype(jnp.bfloat16)


def solution(mesh):
    return jax.shard_map(
        shards,
        mesh=mesh,
        in_specs=(
            P("ctx", "head"),
            P("ctx", "head"),
            P("ctx", "head"),
            P("head", None, None),
            P("head"),
            P("head"),
            P("ctx", None),
            P(),
        ),
        out_specs=P("ctx", "head"),
        check_vma=False,
    )
```

time: 600 us -> 80.4 us (0.13)
  blocking collectives: 235 us -> 15.8 us
  other arithmetic: 141 us -> 3.7 us
  waiting for transfers between devices: 153 us -> 35.1 us
  between operations: 15.7 us -> 0.21 us
  local copies, waits for them, and re-layouts: 18 us -> 4.08 us
    unnamed x1 -> x0, blocking collectives: 222 us -> none
    all_gather x1 -> x0, waiting for transfers between devices: 148 us -> none  [entering(): everything = jax.tree.map(lambda part: lax.all_gather(part, axis), value)]
    select_n x130 -> x4, other arithmetic: 136 us -> 0.17 us  [the longest x1 0.08 us: shards(): jnp.where(at_end[:, None], jnp.exp(-rates[None, :] * (row_count - 1 - win...]
    ppermute x2 -> x4, waiting for transfers between devices: 4.44 us -> 35.1 us  [shifted(): return lax.ppermute(value, axis, pairs)]
    gather x7 -> x0, local copies, waits for them, and re-layouts: 9.29 us -> none  [the longest x2 2.16 us: shards(): ctx_value = jnp.concatenate([value_rows[kept_rows], arrived[2]], axis=0)]
    ppermute x2 -> x4, starting transfers between devices: 23.6 us -> 18.7 us  [shifted(): return lax.ppermute(value, axis, pairs)]
  transfers between devices with their start and end apart: 3 -> 4, of which waited for: 2 -> 4; matrix products, arithmetic and copies ran while one was open for 2% -> 2% of each run, Pallas kernels for 0% -> 0%
where the time goes in v1:
time: 80.4 us; the launch traced here: 80.1 us
  waiting for transfers between devices  35.1 us (44%)
  starting transfers between devices  18.7 us (23%)
  blocking collectives  15.8 us (20%)
  local copies, waits for them, and re-layouts  4.08 us (5%)
  other arithmetic  3.7 us (5%)
  matrix products  2.42 us (3%)
    ppermute x4, waiting for transfers between devices, shifted(): return lax.ppermute(value, axis, pairs)  35.1 us
    ppermute x4, starting transfers between devices, shifted(): return lax.ppermute(value, axis, pairs)  18.7 us
    psum x1, blocking collectives, shards(): square_total = lax.psum(jnp.sum(flat * flat, axis=1), 'head')  15.8 us
    unnamed x14, local copies, waits for them, and re-layouts  2.55 us
  transfers between devices with their start and end apart: 4, of which 4 were waited for; matrix products, arithmetic and copies ran while one was open for 2% of the time, Pallas kernels for 0%

profile of v1, /device:TPU:1, one launch (start us, length us, event | category | flops | bytes accessed | tf_op | source)
XLA Modules:
  0.0 80.1 jit_solution(9934876121877951465)
XLA Ops:
  0.0 0.0 copy-start
  0.1 0.0 copy-start.6
  0.1 0.7 copy-done.6
  0.7 0.0 copy-start.5
  0.8 0.7 copy-done.5
  1.4 0.3 reduce-window.9
  1.7 0.1 slice.28
  1.8 0.1 slice_reduce_fusion
  2.0 0.7 fusion.25
  2.7 0.2 convert_reduce_fusion.2
  2.9 0.1 exponential_select_fusion.3
  3.0 0.0 copy-start.4
  3.0 0.7 copy-done.4
  3.7 0.1 select_reduce_fusion
  3.8 0.2 convert_reduce_fusion
  4.0 0.0 copy-start.1
  4.0 0.0 copy-start.2
  4.0 1.1 %copy.37 = bf16[256,512]{0,1:T(8,128)(2,1)S(1)} copy(bf16[256,512]{1,0:T(8,128)(2,1)} %param.9) | data formatting | bytes 524288 | tf_op jit(solution)/shard_map/reshape | solution.py:56
  5.1 0.7 broadcast_compare_fusion.1
  5.8 0.1 exponential_select_fusion.2
  5.9 0.0 copy-done.1
  5.9 0.0 copy-done.2
  5.9 0.4 convolution_add_fusion
  6.3 4.0 %collective-permute-start = (f32[4,128,128]{2,1,0:T(8,128)S(1)}, f32[4,128,128]{2,1,0:T(8,128)S(1)}, u32[]{:S(2)}, u32[]{:S(2)}) collective-permute-start(f32[4,128,128]{2,1,0:T(8,128)S(1)} %convolution_add_fusion), channel_id=1, source_target_pairs={{0,8},{8,16},{16,24},{24,32},{32,40},{40,48},{48,56},{56,64},{64,7... | collective-permute-start | bytes 786440 | tf_op jit(solution)/shard_map/ppermute | solution.py:11
  10.4 0.1 fusion.16
  10.5 0.1 fusion.7
  10.7 0.0 copy-done
  10.7 0.4 fusion.4
  11.1 2.6 %collective-permute-done = f32[4,128,128]{2,1,0:T(8,128)S(1)} collective-permute-done((f32[4,128,128]{2,1,0:T(8,128)S(1)}, f32[4,128,128]{2,1,0:T(8,128)S(1)}, u32[]{:S(2)}, u32[]{:S(2)}) %collective-permute-start) | collective-permute-done | bytes 262176 | tf_op jit(solution)/shard_map/ppermute | solution.py:11
  13.7 0.1 multiply_add_fusion.1
  13.8 7.4 %collective-permute-start.1 = (f32[4,128,128]{2,1,0:T(8,128)S(1)}, f32[4,128,128]{2,1,0:T(8,128)S(1)}, u32[]{:S(2)}, u32[]{:S(2)}) collective-permute-start(f32[4,128,128]{2,1,0:T(8,128)S(1)} %multiply_add_fusion.1), channel_id=1, source_target_pairs={{0,16},{8,24},{16,32},{24,40},{32,48},{40,56},{48,64},{56,72},{64,... | collective-permute-start | bytes 786440 | tf_op jit(solution)/shard_map/ppermute | solution.py:11
  21.2 0.3 fusion
  21.5 5.0 %collective-permute-done.1 = f32[4,128,128]{2,1,0:T(8,128)S(1)} collective-permute-done((f32[4,128,128]{2,1,0:T(8,128)S(1)}, f32[4,128,128]{2,1,0:T(8,128)S(1)}, u32[]{:S(2)}, u32[]{:S(2)}) %collective-permute-start.1) | collective-permute-done | bytes 262176 | tf_op jit(solution)/shard_map/ppermute | solution.py:11
  26.5 0.1 multiply_add_fusion
  26.6 1.9 %collective-permute-start.3 = (f32[4,128,128]{2,1,0:T(8,128)S(1)}, f32[4,128,128]{2,1,0:T(8,128)S(1)}, u32[]{:S(2)}, u32[]{:S(2)}) collective-permute-start(f32[4,128,128]{2,1,0:T(8,128)S(1)} %multiply_add_fusion), channel_id=1, source_target_pairs={{0,8},{8,16},{16,24},{24,32},{32,40},{40,48},{48,56},{56,64},{64,7... | collective-permute-start | bytes 786440 | tf_op jit(solution)/shard_map/ppermute | solution.py:11
  28.5 5.3 %collective-permute-start.2 = (f32[4,128,128]{2,1,0:T(8,128)S(1)}, f32[4,128,128]{2,1,0:T(8,128)S(1)}, u32[]{:S(2)}, u32[]{:S(2)}) collective-permute-start(f32[4,128,128]{2,1,0:T(8,128)S(1)} %multiply_add_fusion), channel_id=1, source_target_pairs={{0,40},{8,48},{16,56},{24,64},{32,72},{40,80},{48,88},{56,96},{64,... | collective-permute-start | bytes 786440 | tf_op jit(solution)/shard_map/ppermute | solution.py:11
  33.9 0.7 convolution_bitcast_fusion.2
  34.6 16.5 %collective-permute-done.3 = f32[4,128,128]{2,1,0:T(8,128)S(1)} collective-permute-done((f32[4,128,128]{2,1,0:T(8,128)S(1)}, f32[4,128,128]{2,1,0:T(8,128)S(1)}, u32[]{:S(2)}, u32[]{:S(2)}) %collective-permute-start.3) | collective-permute-done | bytes 262176 | tf_op jit(solution)/shard_map/ppermute | solution.py:11
  51.1 11.1 %collective-permute-done.2 = f32[4,128,128]{2,1,0:T(8,128)S(1)} collective-permute-done((f32[4,128,128]{2,1,0:T(8,128)S(1)}, f32[4,128,128]{2,1,0:T(8,128)S(1)}, u32[]{:S(2)}, u32[]{:S(2)}) %collective-permute-start.2) | collective-permute-done | bytes 262176 | tf_op jit(solution)/shard_map/ppermute | solution.py:11
  62.2 0.5 multiply_reduce_fusion
  62.7 15.8 %psum.7 = f32[256]{0:T(256)S(1)} all-reduce(f32[256]{0:T(256)S(1)} %get-tuple-element.21), channel_id=1, replica_groups=mesh['ctx'=128,'head'=8] {'head'}, use_global_device_ids=true, to_apply=%region_8.9 | all-reduce | flops 256 | bytes 2048 | tf_op jit(solution)/shard_map/psum | solution.py:103
  78.5 0.0 copy-start.3
  78.6 0.2 copy.34
  78.8 0.5 copy-done.3
  79.2 0.8 %multiply_convert_fusion = bf16[256,512]{1,0:T(8,128)(2,1)} fusion(f32[256,512]{1,0:T(8,128)S(1)} %copy.34, f32[512]{0:T(512)S(1)} %copy-done.3, f32[256]{0:T(256)S(1)} %add_rsqrt_fusion), kind=kLoop, calls=%fused_computation.10 | loop fusion | flops 393216 | bytes 789504 | tf_op jit(solution)/shard_map/convert_element_type | solution.py:105
  (10 shorter events, 0.1 us)
Async XLA Ops:
  0.0 10.7 %copy-start = (bf16[256,512]{1,0:T(8,128)(2,1)S(1)}, bf16[256,512]{1,0:T(8,128)(2,1)}, u32[]{:S(2)}) copy-start(bf16[256,512]{1,0:T(8,128)(2,1)} %param.8) | copy-start | bytes 786436
  0.1 0.7 copy-start.6
  0.7 0.7 copy-start.5
  3.0 0.7 copy-start.4
  4.0 1.9 %copy-start.1 = (bf16[256,512]{1,0:T(8,128)(2,1)S(1)}, bf16[256,512]{1,0:T(8,128)(2,1)}, u32[]{:S(2)}) copy-start(bf16[256,512]{1,0:T(8,128)(2,1)} %param.10) | copy-start | bytes 786436
  4.0 1.9 %copy-start.2 = (f32[4,128,128]{2,1,0:T(8,128)S(1)}, f32[4,128,128]{2,1,0:T(8,128)}, u32[]{:S(2)}) copy-start(f32[4,128,128]{2,1,0:T(8,128)} %param.11) | copy-start | bytes 786436
  6.3 7.3 %collective-permute-start = (f32[4,128,128]{2,1,0:T(8,128)S(1)}, f32[4,128,128]{2,1,0:T(8,128)S(1)}, u32[]{:S(2)}, u32[]{:S(2)}) collective-permute-start(f32[4,128,128]{2,1,0:T(8,128)S(1)} %convolution_add_fusion), channel_id=1, source_target_pairs={{0,8},{8,16},{16,24},{24,32},{32,40},{40,48},{48,56},{56,64},{64,7... | collective-permute-start | bytes 786440 | tf_op jit(solution)/shard_map/ppermute | solution.py:11
  13.8 12.7 %collective-permute-start.1 = (f32[4,128,128]{2,1,0:T(8,128)S(1)}, f32[4,128,128]{2,1,0:T(8,128)S(1)}, u32[]{:S(2)}, u32[]{:S(2)}) collective-permute-start(f32[4,128,128]{2,1,0:T(8,128)S(1)} %multiply_add_fusion.1), channel_id=1, source_target_pairs={{0,16},{8,24},{16,32},{24,40},{32,48},{40,56},{48,64},{56,72},{64,... | collective-permute-start | bytes 786440 | tf_op jit(solution)/shard_map/ppermute | solution.py:11
  26.6 24.5 %collective-permute-start.3 = (f32[4,128,128]{2,1,0:T(8,128)S(1)}, f32[4,128,128]{2,1,0:T(8,128)S(1)}, u32[]{:S(2)}, u32[]{:S(2)}) collective-permute-start(f32[4,128,128]{2,1,0:T(8,128)S(1)} %multiply_add_fusion), channel_id=1, source_target_pairs={{0,8},{8,16},{16,24},{24,32},{32,40},{40,48},{48,56},{56,64},{64,7... | collective-permute-start | bytes 786440 | tf_op jit(solution)/shard_map/ppermute | solution.py:11
  28.5 33.6 %collective-permute-start.2 = (f32[4,128,128]{2,1,0:T(8,128)S(1)}, f32[4,128,128]{2,1,0:T(8,128)S(1)}, u32[]{:S(2)}, u32[]{:S(2)}) collective-permute-start(f32[4,128,128]{2,1,0:T(8,128)S(1)} %multiply_add_fusion), channel_id=1, source_target_pairs={{0,40},{8,48},{16,56},{24,64},{32,72},{40,80},{48,88},{56,96},{64,... | collective-permute-start | bytes 786440 | tf_op jit(solution)/shard_map/ppermute | solution.py:11
  78.5 0.7 copy-start.3

commit v2 on v1

--- a/solution.py
+++ b/solution.py
@@ -69,14 +69,20 @@
     initial = carry_state * (device == 0).astype(jnp.float32)
     element = through[0][:, None, None] * initial + running
 
-    got = shifted(element, "ctx", 1)
-    pair = through[0][:, None, None] * got + element
-    got = shifted(pair, "ctx", 2)
-    quad = (through[0] * through[1])[:, None, None] * got + pair
-    near_quad = shifted(quad, "ctx", 1, wrap_sources=(ctx_count - 1,))
-    far_quad = shifted(quad, "ctx", 5, wrap_sources=(ctx_count - 5,))
-    span4 = through[1] * through[2] * through[3] * through[4]
-    incoming = span4[:, None, None] * far_quad + near_quad
+    last = ctx_count - 1
+    e1 = shifted(element, "ctx", 1, wrap_sources=(last,))
+    e2 = shifted(element, "ctx", 2, wrap_sources=(last - 1,))
+    e3 = shifted(element, "ctx", 3, wrap_sources=(last - 2,))
+    e4 = shifted(element, "ctx", 4)
+    t0, t1, t2, t3 = (through[i][:, None, None] for i in range(4))
+    inner = (device != 0).astype(jnp.float32)
+    reach1 = t0 * inner
+    reach2 = reach1 * t1
+    reach3 = reach2 * t2
+    five = element + reach1 * e1 + reach2 * e2 + reach3 * e3 + reach3 * t3 * e4
+    three = e1 + t1 * e2 + t1 * t2 * e3
+    far = shifted(five, "ctx", 4, wrap_sources=(last - 3,))
+    incoming = three + t1 * t2 * t3 * far
 
     distance = window[:, None] - window[None, :]
     same_doc = (segment[:, None] == segment[None, :]) & (distance >= 0)

time: 80.4 us -> 75.2 us (0.935)
  blocking collectives: 15.8 us -> 14 us
  starting transfers between devices: 18.7 us -> 17.2 us
  waiting for transfers between devices: 35.1 us -> 33.7 us
    psum x1, blocking collectives: 15.8 us -> 14 us  [shards(): square_total = lax.psum(jnp.sum(flat * flat, axis=1), 'head')]
    ppermute x4 -> x5, starting transfers between devices: 18.7 us -> 17.2 us  [shifted(): return lax.ppermute(value, axis, pairs)]
    ppermute x4 -> x5, waiting for transfers between devices: 35.1 us -> 33.7 us  [shifted(): return lax.ppermute(value, axis, pairs)]
  transfers between devices with their start and end apart: 4 -> 5, of which waited for: 4 -> 4; matrix products, arithmetic and copies ran while one was open for 2% -> 2% of each run, Pallas kernels for 0% -> 0%
where the time goes in v2:
time: 75.2 us; the launch traced here: 74.9 us
  waiting for transfers between devices  33.7 us (45%)
  starting transfers between devices  17.2 us (23%)
  blocking collectives  14 us (19%)
  other arithmetic  3.68 us (5%)
  local copies, waits for them, and re-layouts  3.59 us (5%)
  matrix products  2.43 us (3%)
    ppermute x5, waiting for transfers between devices, shifted(): return lax.ppermute(value, axis, pairs)  33.7 us
    ppermute x5, starting transfers between devices, shifted(): return lax.ppermute(value, axis, pairs)  17.2 us
    psum x1, blocking collectives, shards(): square_total = lax.psum(jnp.sum(flat * flat, axis=1), 'head')  14 us
    unnamed x14, local copies, waits for them, and re-layouts  2.05 us
  transfers between devices with their start and end apart: 5, of which 4 were waited for; matrix products, arithmetic and copies ran while one was open for 2% of the time, Pallas kernels for 0%

profile of v2, /device:TPU:1, one launch (start us, length us, event | category | flops | bytes accessed | tf_op | source)
XLA Modules:
  0.0 74.9 jit_solution(13856561249971438247)
XLA Ops:
  0.0 0.0 copy-start
  0.1 0.0 copy-start.6
  0.1 0.7 copy-done.6
  0.8 0.0 copy-start.5
  0.8 0.7 copy-done.5
  1.4 0.3 reduce-window.9
  1.7 0.1 slice.23
  1.9 0.1 slice_reduce_fusion
  2.0 0.0 copy-start.1
  2.0 0.0 copy-start.2
  2.0 1.1 %copy.37 = bf16[256,512]{0,1:T(8,128)(2,1)S(1)} copy(bf16[256,512]{1,0:T(8,128)(2,1)} %param.9) | data formatting | bytes 524288 | tf_op jit(solution)/shard_map/reshape | solution.py:56
  3.1 0.0 copy-start.4
  3.2 0.7 copy-done.4
  3.8 0.1 select_reduce_fusion
  4.0 0.7 fusion.31
  4.7 0.2 convert_reduce_fusion
  4.8 0.2 convert_reduce_fusion.2
  5.1 0.1 exponential_select_fusion.3
  5.2 0.7 broadcast_compare_fusion.1
  5.9 0.1 exponential_select_fusion.2
  5.9 0.0 copy-done.1
  6.0 0.0 copy-done.2
  6.0 0.4 convolution_add_fusion
  6.4 4.4 %collective-permute-start.3 = (f32[4,128,128]{2,1,0:T(8,128)S(1)}, f32[4,128,128]{2,1,0:T(8,128)S(1)}, u32[]{:S(2)}, u32[]{:S(2)}) collective-permute-start(f32[4,128,128]{2,1,0:T(8,128)S(1)} %convolution_add_fusion), channel_id=1, source_target_pairs={{0,32},{8,40},{16,48},{24,56},{32,64},{40,72},{48,80},{56,88},{64,... | collective-permute-start | bytes 786440 | tf_op jit(solution)/shard_map/ppermute | solution.py:11
  10.8 4.6 %collective-permute-start.2 = (f32[4,128,128]{2,1,0:T(8,128)S(1)}, f32[4,128,128]{2,1,0:T(8,128)S(1)}, u32[]{:S(2)}, u32[]{:S(2)}) collective-permute-start(f32[4,128,128]{2,1,0:T(8,128)S(1)} %convolution_add_fusion), channel_id=1, source_target_pairs={{0,24},{8,32},{16,40},{24,48},{32,56},{40,64},{48,72},{56,80},{64,... | collective-permute-start | bytes 786440 | tf_op jit(solution)/shard_map/ppermute | solution.py:11
  15.4 3.6 %collective-permute-start.1 = (f32[4,128,128]{2,1,0:T(8,128)S(1)}, f32[4,128,128]{2,1,0:T(8,128)S(1)}, u32[]{:S(2)}, u32[]{:S(2)}) collective-permute-start(f32[4,128,128]{2,1,0:T(8,128)S(1)} %convolution_add_fusion), channel_id=1, source_target_pairs={{0,16},{8,24},{16,32},{24,40},{32,48},{40,56},{48,64},{56,72},{64,... | collective-permute-start | bytes 786440 | tf_op jit(solution)/shard_map/ppermute | solution.py:11
  19.0 2.6 %collective-permute-start = (f32[4,128,128]{2,1,0:T(8,128)S(1)}, f32[4,128,128]{2,1,0:T(8,128)S(1)}, u32[]{:S(2)}, u32[]{:S(2)}) collective-permute-start(f32[4,128,128]{2,1,0:T(8,128)S(1)} %convolution_add_fusion), channel_id=1, source_target_pairs={{0,8},{8,16},{16,24},{24,32},{32,40},{40,48},{48,56},{56,64},{64,7... | collective-permute-start | bytes 786440 | tf_op jit(solution)/shard_map/ppermute | solution.py:11
  21.6 0.1 fusion.7
  21.7 0.1 fusion.20
  21.9 0.0 copy-done
  21.9 0.4 fusion.4
  22.4 0.3 fusion
  22.7 0.0 collective-permute-done.3
  22.7 11.2 %collective-permute-done.2 = f32[4,128,128]{2,1,0:T(8,128)S(1)} collective-permute-done((f32[4,128,128]{2,1,0:T(8,128)S(1)}, f32[4,128,128]{2,1,0:T(8,128)S(1)}, u32[]{:S(2)}, u32[]{:S(2)}) %collective-permute-start.2) | collective-permute-done | bytes 262176 | tf_op jit(solution)/shard_map/ppermute | solution.py:11
  33.9 6.5 %collective-permute-done.1 = f32[4,128,128]{2,1,0:T(8,128)S(1)} collective-permute-done((f32[4,128,128]{2,1,0:T(8,128)S(1)}, f32[4,128,128]{2,1,0:T(8,128)S(1)}, u32[]{:S(2)}, u32[]{:S(2)}) %collective-permute-start.1) | collective-permute-done | bytes 262176 | tf_op jit(solution)/shard_map/ppermute | solution.py:11
  40.5 1.7 %collective-permute-done = f32[4,128,128]{2,1,0:T(8,128)S(1)} collective-permute-done((f32[4,128,128]{2,1,0:T(8,128)S(1)}, f32[4,128,128]{2,1,0:T(8,128)S(1)}, u32[]{:S(2)}, u32[]{:S(2)}) %collective-permute-start) | collective-permute-done | bytes 262176 | tf_op jit(solution)/shard_map/ppermute | solution.py:11
  42.1 0.1 multiply_add_fusion
  42.3 1.9 %collective-permute-start.4 = (f32[4,128,128]{2,1,0:T(8,128)S(1)}, f32[4,128,128]{2,1,0:T(8,128)S(1)}, u32[]{:S(2)}, u32[]{:S(2)}) collective-permute-start(f32[4,128,128]{2,1,0:T(8,128)S(1)} %multiply_add_fusion), channel_id=1, source_target_pairs={{0,32},{8,40},{16,48},{24,56},{32,64},{40,72},{48,80},{56,88},{64,... | collective-permute-start | bytes 786440 | tf_op jit(solution)/shard_map/ppermute | solution.py:11
  44.2 0.7 convolution_bitcast_fusion.2
  44.9 14.3 %collective-permute-done.4 = f32[4,128,128]{2,1,0:T(8,128)S(1)} collective-permute-done((f32[4,128,128]{2,1,0:T(8,128)S(1)}, f32[4,128,128]{2,1,0:T(8,128)S(1)}, u32[]{:S(2)}, u32[]{:S(2)}) %collective-permute-start.4) | collective-permute-done | bytes 262176 | tf_op jit(solution)/shard_map/ppermute | solution.py:11
  59.2 0.6 multiply_reduce_fusion
  59.8 0.2 copy.34
  60.0 0.0 copy-start.3
  60.0 14.0 %psum.7 = f32[256]{0:T(256)S(1)} all-reduce(f32[256]{0:T(256)S(1)} %get-tuple-element.31), channel_id=1, replica_groups=mesh['ctx'=128,'head'=8] {'head'}, use_global_device_ids=true, to_apply=%region_8.9 | all-reduce | flops 256 | bytes 2048 | tf_op jit(solution)/shard_map/psum | solution.py:109
  74.1 0.0 copy-done.3
  74.1 0.8 %multiply_convert_fusion = bf16[256,512]{1,0:T(8,128)(2,1)} fusion(f32[256,512]{1,0:T(8,128)S(1)} %copy.34, f32[512]{0:T(512)S(1)} %copy-done.3, f32[256]{0:T(256)S(1)} %add_rsqrt_fusion), kind=kLoop, calls=%fused_computation.10 | loop fusion | flops 393216 | bytes 789504 | tf_op jit(solution)/shard_map/convert_element_type | solution.py:111
  (10 shorter events, 0.1 us)
Async XLA Ops:
  0.0 21.9 %copy-start = (bf16[256,512]{1,0:T(8,128)(2,1)S(1)}, bf16[256,512]{1,0:T(8,128)(2,1)}, u32[]{:S(2)}) copy-start(bf16[256,512]{1,0:T(8,128)(2,1)} %param.8) | copy-start | bytes 786436
  0.1 0.7 copy-start.6
  0.8 0.7 copy-start.5
  2.0 4.0 %copy-start.1 = (bf16[256,512]{1,0:T(8,128)(2,1)S(1)}, bf16[256,512]{1,0:T(8,128)(2,1)}, u32[]{:S(2)}) copy-start(bf16[256,512]{1,0:T(8,128)(2,1)} %param.10) | copy-start | bytes 786436
  2.0 4.0 %copy-start.2 = (f32[4,128,128]{2,1,0:T(8,128)S(1)}, f32[4,128,128]{2,1,0:T(8,128)}, u32[]{:S(2)}) copy-start(f32[4,128,128]{2,1,0:T(8,128)} %param.11) | copy-start | bytes 786436
  3.1 0.7 copy-start.4
  6.4 16.3 %collective-permute-start.3 = (f32[4,128,128]{2,1,0:T(8,128)S(1)}, f32[4,128,128]{2,1,0:T(8,128)S(1)}, u32[]{:S(2)}, u32[]{:S(2)}) collective-permute-start(f32[4,128,128]{2,1,0:T(8,128)S(1)} %convolution_add_fusion), channel_id=1, source_target_pairs={{0,32},{8,40},{16,48},{24,56},{32,64},{40,72},{48,80},{56,88},{64,... | collective-permute-start | bytes 786440 | tf_op jit(solution)/shard_map/ppermute | solution.py:11
  10.8 23.2 %collective-permute-start.2 = (f32[4,128,128]{2,1,0:T(8,128)S(1)}, f32[4,128,128]{2,1,0:T(8,128)S(1)}, u32[]{:S(2)}, u32[]{:S(2)}) collective-permute-start(f32[4,128,128]{2,1,0:T(8,128)S(1)} %convolution_add_fusion), channel_id=1, source_target_pairs={{0,24},{8,32},{16,40},{24,48},{32,56},{40,64},{48,72},{56,80},{64,... | collective-permute-start | bytes 786440 | tf_op jit(solution)/shard_map/ppermute | solution.py:11
  15.4 25.0 %collective-permute-start.1 = (f32[4,128,128]{2,1,0:T(8,128)S(1)}, f32[4,128,128]{2,1,0:T(8,128)S(1)}, u32[]{:S(2)}, u32[]{:S(2)}) collective-permute-start(f32[4,128,128]{2,1,0:T(8,128)S(1)} %convolution_add_fusion), channel_id=1, source_target_pairs={{0,16},{8,24},{16,32},{24,40},{32,48},{40,56},{48,64},{56,72},{64,... | collective-permute-start | bytes 786440 | tf_op jit(solution)/shard_map/ppermute | solution.py:11
  19.0 23.1 %collective-permute-start = (f32[4,128,128]{2,1,0:T(8,128)S(1)}, f32[4,128,128]{2,1,0:T(8,128)S(1)}, u32[]{:S(2)}, u32[]{:S(2)}) collective-permute-start(f32[4,128,128]{2,1,0:T(8,128)S(1)} %convolution_add_fusion), channel_id=1, source_target_pairs={{0,8},{8,16},{16,24},{24,32},{32,40},{40,48},{48,56},{56,64},{64,7... | collective-permute-start | bytes 786440 | tf_op jit(solution)/shard_map/ppermute | solution.py:11
  42.3 17.0 %collective-permute-start.4 = (f32[4,128,128]{2,1,0:T(8,128)S(1)}, f32[4,128,128]{2,1,0:T(8,128)S(1)}, u32[]{:S(2)}, u32[]{:S(2)}) collective-permute-start(f32[4,128,128]{2,1,0:T(8,128)S(1)} %multiply_add_fusion), channel_id=1, source_target_pairs={{0,32},{8,40},{16,48},{24,56},{32,64},{40,72},{48,80},{56,88},{64,... | collective-permute-start | bytes 786440 | tf_op jit(solution)/shard_map/ppermute | solution.py:11
  60.0 14.0 %copy-start.3 = (f32[512]{0:T(512)S(1)}, f32[512]{0:T(512)}, u32[]{:S(2)}) copy-start(f32[512]{0:T(512)} %param.13) | copy-start | bytes 6148

commit v3 on v2

--- a/solution.py
+++ b/solution.py
@@ -106,25 +106,29 @@
     attn = attn + carried * lead_in[:, :, None] + started * lead_init[:, :, None]
 
     flat = attn.reshape(row_count, feature_count)
-    square_total = lax.psum(jnp.sum(flat * flat, axis=1), "head")
-    mean_sq = square_total / jnp.float32(feature_count * lax.axis_size("head"))
+    square_total = lax.psum(lax.psum(jnp.sum(flat * flat, axis=1), "core"), "chip")
+    mean_sq = square_total / jnp.float32(feature_count * lax.axis_size("chip") * lax.axis_size("core"))
     return (flat * lax.rsqrt(mean_sq + 1e-05)[:, None] * norm_gain[None, :]).astype(jnp.bfloat16)
 
 
 def solution(mesh):
+    split = jax.sharding.Mesh(
+        mesh.devices.reshape(mesh.shape["ctx"], mesh.shape["head"] // 2, 2), ("ctx", "chip", "core")
+    )
+    head = ("chip", "core")
     return jax.shard_map(
         shards,
-        mesh=mesh,
+        mesh=split,
         in_specs=(
-            P("ctx", "head"),
-            P("ctx", "head"),
-            P("ctx", "head"),
-            P("head", None, None),
-            P("head"),
-            P("head"),
+            P("ctx", head),
+            P("ctx", head),
+            P("ctx", head),
+            P(head, None, None),
+            P(head),
+            P(head),
             P("ctx", None),
             P(),
         ),
-        out_specs=P("ctx", "head"),
+        out_specs=P("ctx", head),
         check_vma=False,
     )

time: 75.2 us -> 74.2 us (0.987)
  blocking collectives: 14 us -> 12.9 us
    psum x1 -> x2, blocking collectives: 14 us -> 12.9 us  [the longest x1 8.57 us: shards(): lax.psum(lax.psum(jnp.sum(flat * flat, axis=1), 'core'), 'chip')]
where the time goes in v3:
time: 74.2 us; the launch traced here: 73.8 us
  waiting for transfers between devices  33.7 us (45%)
  starting transfers between devices  17.2 us (23%)
  blocking collectives  12.9 us (17%)
  other arithmetic  3.68 us (5%)
  local copies, waits for them, and re-layouts  3.58 us (5%)
  matrix products  2.43 us (3%)
    ppermute x5, waiting for transfers between devices, shifted(): return lax.ppermute(value, axis, pairs)  33.7 us
    ppermute x5, starting transfers between devices, shifted(): return lax.ppermute(value, axis, pairs)  17.2 us
    psum x1, blocking collectives, shards(): lax.psum(lax.psum(jnp.sum(flat * flat, axis=1), 'core'), 'chip')  8.57 us
    psum x1, blocking collectives, shards(): lax.psum(jnp.sum(flat * flat, axis=1), 'core')  4.37 us
    unnamed x14, local copies, waits for them, and re-layouts  2.05 us
  transfers between devices with their start and end apart: 5, of which 4 were waited for; matrix products, arithmetic and copies ran while one was open for 2% of the time, Pallas kernels for 0%

profile of v3, /device:TPU:1, one launch (start us, length us, event | category | flops | bytes accessed | tf_op | source)
XLA Modules:
  0.0 73.8 jit_solution(6074946789546594940)
XLA Ops:
  0.0 0.0 copy-start
  0.1 0.0 copy-start.6
  0.1 0.7 copy-done.6
  0.8 0.0 copy-start.5
  0.8 0.7 copy-done.5
  1.4 0.3 reduce-window.9
  1.7 0.1 slice.23
  1.9 0.1 slice_reduce_fusion
  2.0 0.0 copy-start.1
  2.0 0.0 copy-start.2
  2.0 1.1 %copy.37 = bf16[256,512]{0,1:T(8,128)(2,1)S(1)} copy(bf16[256,512]{1,0:T(8,128)(2,1)} %param.9) | data formatting | bytes 524288 | tf_op jit(solution)/shard_map/reshape | solution.py:56
  3.1 0.0 copy-start.4
  3.2 0.7 copy-done.4
  3.8 0.1 select_reduce_fusion
  4.0 0.7 fusion.31
  4.7 0.2 convert_reduce_fusion
  4.8 0.2 convert_reduce_fusion.2
  5.1 0.1 exponential_select_fusion.3
  5.2 0.7 broadcast_compare_fusion.1
  5.9 0.1 exponential_select_fusion.2
  5.9 0.0 copy-done.1
  6.0 0.0 copy-done.2
  6.0 0.4 convolution_add_fusion
  6.4 4.4 %collective-permute-start.3 = (f32[4,128,128]{2,1,0:T(8,128)S(1)}, f32[4,128,128]{2,1,0:T(8,128)S(1)}, u32[]{:S(2)}, u32[]{:S(2)}) collective-permute-start(f32[4,128,128]{2,1,0:T(8,128)S(1)} %convolution_add_fusion), channel_id=1, source_target_pairs={{0,32},{8,40},{16,48},{24,56},{32,64},{40,72},{48,80},{56,88},{64,... | collective-permute-start | bytes 786440 | tf_op jit(solution)/shard_map/ppermute | solution.py:11
  10.8 4.6 %collective-permute-start.2 = (f32[4,128,128]{2,1,0:T(8,128)S(1)}, f32[4,128,128]{2,1,0:T(8,128)S(1)}, u32[]{:S(2)}, u32[]{:S(2)}) collective-permute-start(f32[4,128,128]{2,1,0:T(8,128)S(1)} %convolution_add_fusion), channel_id=1, source_target_pairs={{0,24},{8,32},{16,40},{24,48},{32,56},{40,64},{48,72},{56,80},{64,... | collective-permute-start | bytes 786440 | tf_op jit(solution)/shard_map/ppermute | solution.py:11
  15.4 3.6 %collective-permute-start.1 = (f32[4,128,128]{2,1,0:T(8,128)S(1)}, f32[4,128,128]{2,1,0:T(8,128)S(1)}, u32[]{:S(2)}, u32[]{:S(2)}) collective-permute-start(f32[4,128,128]{2,1,0:T(8,128)S(1)} %convolution_add_fusion), channel_id=1, source_target_pairs={{0,16},{8,24},{16,32},{24,40},{32,48},{40,56},{48,64},{56,72},{64,... | collective-permute-start | bytes 786440 | tf_op jit(solution)/shard_map/ppermute | solution.py:11
  19.0 2.6 %collective-permute-start = (f32[4,128,128]{2,1,0:T(8,128)S(1)}, f32[4,128,128]{2,1,0:T(8,128)S(1)}, u32[]{:S(2)}, u32[]{:S(2)}) collective-permute-start(f32[4,128,128]{2,1,0:T(8,128)S(1)} %convolution_add_fusion), channel_id=1, source_target_pairs={{0,8},{8,16},{16,24},{24,32},{32,40},{40,48},{48,56},{56,64},{64,7... | collective-permute-start | bytes 786440 | tf_op jit(solution)/shard_map/ppermute | solution.py:11
  21.6 0.1 fusion.7
  21.7 0.1 fusion.20
  21.9 0.0 copy-done
  21.9 0.4 fusion.4
  22.4 0.3 fusion
  22.7 0.0 collective-permute-done.3
  22.7 11.2 %collective-permute-done.2 = f32[4,128,128]{2,1,0:T(8,128)S(1)} collective-permute-done((f32[4,128,128]{2,1,0:T(8,128)S(1)}, f32[4,128,128]{2,1,0:T(8,128)S(1)}, u32[]{:S(2)}, u32[]{:S(2)}) %collective-permute-start.2) | collective-permute-done | bytes 262176 | tf_op jit(solution)/shard_map/ppermute | solution.py:11
  33.9 6.5 %collective-permute-done.1 = f32[4,128,128]{2,1,0:T(8,128)S(1)} collective-permute-done((f32[4,128,128]{2,1,0:T(8,128)S(1)}, f32[4,128,128]{2,1,0:T(8,128)S(1)}, u32[]{:S(2)}, u32[]{:S(2)}) %collective-permute-start.1) | collective-permute-done | bytes 262176 | tf_op jit(solution)/shard_map/ppermute | solution.py:11
  40.5 1.7 %collective-permute-done = f32[4,128,128]{2,1,0:T(8,128)S(1)} collective-permute-done((f32[4,128,128]{2,1,0:T(8,128)S(1)}, f32[4,128,128]{2,1,0:T(8,128)S(1)}, u32[]{:S(2)}, u32[]{:S(2)}) %collective-permute-start) | collective-permute-done | bytes 262176 | tf_op jit(solution)/shard_map/ppermute | solution.py:11
  42.1 0.1 multiply_add_fusion
  42.3 1.9 %collective-permute-start.4 = (f32[4,128,128]{2,1,0:T(8,128)S(1)}, f32[4,128,128]{2,1,0:T(8,128)S(1)}, u32[]{:S(2)}, u32[]{:S(2)}) collective-permute-start(f32[4,128,128]{2,1,0:T(8,128)S(1)} %multiply_add_fusion), channel_id=1, source_target_pairs={{0,32},{8,40},{16,48},{24,56},{32,64},{40,72},{48,80},{56,88},{64,... | collective-permute-start | bytes 786440 | tf_op jit(solution)/shard_map/ppermute | solution.py:11
  44.2 0.7 convolution_bitcast_fusion.2
  44.9 14.3 %collective-permute-done.4 = f32[4,128,128]{2,1,0:T(8,128)S(1)} collective-permute-done((f32[4,128,128]{2,1,0:T(8,128)S(1)}, f32[4,128,128]{2,1,0:T(8,128)S(1)}, u32[]{:S(2)}, u32[]{:S(2)}) %collective-permute-start.4) | collective-permute-done | bytes 262176 | tf_op jit(solution)/shard_map/ppermute | solution.py:11
  59.2 0.6 multiply_reduce_fusion
  59.8 0.2 copy.34
  60.0 4.4 %psum.14 = f32[256]{0:T(256)S(1)} all-reduce(f32[256]{0:T(256)S(1)} %get-tuple-element.31), channel_id=1, replica_groups=mesh['ctx'=128,'chip'=4,'core'=2] {'core'}, use_global_device_ids=true, to_apply=%region_8.9 | all-reduce | flops 256 | bytes 2048 | tf_op jit(solution)/shard_map/psum | solution.py:109
  64.4 0.0 copy-start.3
  64.4 8.6 %psum.15 = f32[256]{0:T(256)S(1)} all-reduce(f32[256]{0:T(256)S(1)} %psum.14), channel_id=1, replica_groups=mesh['ctx'=128,'chip'=4,'core'=2] {'chip'}, use_global_device_ids=true, to_apply=%region_9.10 | all-reduce | flops 256 | bytes 2048 | tf_op jit(solution)/shard_map/psum | solution.py:109
  73.0 0.0 copy-done.3
  73.0 0.8 %multiply_convert_fusion = bf16[256,512]{1,0:T(8,128)(2,1)} fusion(f32[256,512]{1,0:T(8,128)S(1)} %copy.34, f32[512]{0:T(512)S(1)} %copy-done.3, f32[256]{0:T(256)S(1)} %add_rsqrt_fusion), kind=kLoop, calls=%fused_computation.10 | loop fusion | flops 393216 | bytes 789504 | tf_op jit(solution)/shard_map/convert_element_type | solution.py:111
  (10 shorter events, 0.1 us)
Async XLA Ops:
  0.0 21.9 %copy-start = (bf16[256,512]{1,0:T(8,128)(2,1)S(1)}, bf16[256,512]{1,0:T(8,128)(2,1)}, u32[]{:S(2)}) copy-start(bf16[256,512]{1,0:T(8,128)(2,1)} %param.8) | copy-start | bytes 786436
  0.1 0.7 copy-start.6
  0.8 0.7 copy-start.5
  2.0 4.0 %copy-start.1 = (bf16[256,512]{1,0:T(8,128)(2,1)S(1)}, bf16[256,512]{1,0:T(8,128)(2,1)}, u32[]{:S(2)}) copy-start(bf16[256,512]{1,0:T(8,128)(2,1)} %param.10) | copy-start | bytes 786436
  2.0 4.0 %copy-start.2 = (f32[4,128,128]{2,1,0:T(8,128)S(1)}, f32[4,128,128]{2,1,0:T(8,128)}, u32[]{:S(2)}) copy-start(f32[4,128,128]{2,1,0:T(8,128)} %param.11) | copy-start | bytes 786436
  3.1 0.7 copy-start.4
  6.4 16.3 %collective-permute-start.3 = (f32[4,128,128]{2,1,0:T(8,128)S(1)}, f32[4,128,128]{2,1,0:T(8,128)S(1)}, u32[]{:S(2)}, u32[]{:S(2)}) collective-permute-start(f32[4,128,128]{2,1,0:T(8,128)S(1)} %convolution_add_fusion), channel_id=1, source_target_pairs={{0,32},{8,40},{16,48},{24,56},{32,64},{40,72},{48,80},{56,88},{64,... | collective-permute-start | bytes 786440 | tf_op jit(solution)/shard_map/ppermute | solution.py:11
  10.8 23.2 %collective-permute-start.2 = (f32[4,128,128]{2,1,0:T(8,128)S(1)}, f32[4,128,128]{2,1,0:T(8,128)S(1)}, u32[]{:S(2)}, u32[]{:S(2)}) collective-permute-start(f32[4,128,128]{2,1,0:T(8,128)S(1)} %convolution_add_fusion), channel_id=1, source_target_pairs={{0,24},{8,32},{16,40},{24,48},{32,56},{40,64},{48,72},{56,80},{64,... | collective-permute-start | bytes 786440 | tf_op jit(solution)/shard_map/ppermute | solution.py:11
  15.4 25.0 %collective-permute-start.1 = (f32[4,128,128]{2,1,0:T(8,128)S(1)}, f32[4,128,128]{2,1,0:T(8,128)S(1)}, u32[]{:S(2)}, u32[]{:S(2)}) collective-permute-start(f32[4,128,128]{2,1,0:T(8,128)S(1)} %convolution_add_fusion), channel_id=1, source_target_pairs={{0,16},{8,24},{16,32},{24,40},{32,48},{40,56},{48,64},{56,72},{64,... | collective-permute-start | bytes 786440 | tf_op jit(solution)/shard_map/ppermute | solution.py:11
  19.0 23.1 %collective-permute-start = (f32[4,128,128]{2,1,0:T(8,128)S(1)}, f32[4,128,128]{2,1,0:T(8,128)S(1)}, u32[]{:S(2)}, u32[]{:S(2)}) collective-permute-start(f32[4,128,128]{2,1,0:T(8,128)S(1)} %convolution_add_fusion), channel_id=1, source_target_pairs={{0,8},{8,16},{16,24},{24,32},{32,40},{40,48},{48,56},{56,64},{64,7... | collective-permute-start | bytes 786440 | tf_op jit(solution)/shard_map/ppermute | solution.py:11
  42.3 17.0 %collective-permute-start.4 = (f32[4,128,128]{2,1,0:T(8,128)S(1)}, f32[4,128,128]{2,1,0:T(8,128)S(1)}, u32[]{:S(2)}, u32[]{:S(2)}) collective-permute-start(f32[4,128,128]{2,1,0:T(8,128)S(1)} %multiply_add_fusion), channel_id=1, source_target_pairs={{0,32},{8,40},{16,48},{24,56},{32,64},{40,72},{48,80},{56,88},{64,... | collective-permute-start | bytes 786440 | tf_op jit(solution)/shard_map/ppermute | solution.py:11
  64.4 8.6 %copy-start.3 = (f32[512]{0:T(512)S(1)}, f32[512]{0:T(512)}, u32[]{:S(2)}) copy-start(f32[512]{0:T(512)} %param.13) | copy-start | bytes 6148

commit v4 on v3

--- a/solution.py
+++ b/solution.py
@@ -47,7 +47,7 @@
         )
         return end_seg, through
 
-    near = (device - jnp.arange(5, dtype=jnp.int32)) % ctx_count
+    near = (device - jnp.arange(6, dtype=jnp.int32)) % ctx_count
     end_segs, through = window_bounds(near)
     in_seg = doc_of(((device * row_count - spill_count - 1) % total)[None])[0]
     end_seg = end_segs[0]
@@ -72,17 +72,14 @@
     last = ctx_count - 1
     e1 = shifted(element, "ctx", 1, wrap_sources=(last,))
     e2 = shifted(element, "ctx", 2, wrap_sources=(last - 1,))
-    e3 = shifted(element, "ctx", 3, wrap_sources=(last - 2,))
-    e4 = shifted(element, "ctx", 4)
-    t0, t1, t2, t3 = (through[i][:, None, None] for i in range(4))
-    inner = (device != 0).astype(jnp.float32)
-    reach1 = t0 * inner
-    reach2 = reach1 * t1
-    reach3 = reach2 * t2
-    five = element + reach1 * e1 + reach2 * e2 + reach3 * e3 + reach3 * t3 * e4
-    three = e1 + t1 * e2 + t1 * t2 * e3
-    far = shifted(five, "ctx", 4, wrap_sources=(last - 3,))
-    incoming = three + t1 * t2 * t3 * far
+    t0, t1, t2, t3, t4, t5 = (through[i][:, None, None] for i in range(6))
+    reach1 = t0 * (device != 0).astype(jnp.float32)
+    three = element + reach1 * e1 + reach1 * t1 * e2
+    two = e1 + t1 * e2
+    mid = shifted(three, "ctx", 3, wrap_sources=(last - 2,))
+    far = shifted(three, "ctx", 6, wrap_sources=(last - 5,))
+    span2 = t1 * t2
+    incoming = two + span2 * mid + span2 * t3 * t4 * t5 * far
 
     distance = window[:, None] - window[None, :]
     same_doc = (segment[:, None] == segment[None, :]) & (distance >= 0)

time: 74.2 us -> 74.6 us (level)
  starting transfers between devices: 17.2 us -> 11.8 us
  waiting for transfers between devices: 33.7 us -> 36.8 us
  blocking collectives: 12.9 us -> 15.7 us
    ppermute x5 -> x4, starting transfers between devices: 17.2 us -> 11.8 us  [shifted(): return lax.ppermute(value, axis, pairs)]
    ppermute x5 -> x4, waiting for transfers between devices: 33.7 us -> 36.8 us  [shifted(): return lax.ppermute(value, axis, pairs)]
    psum x1, blocking collectives: 4.37 us -> 7.11 us  [shards(): lax.psum(jnp.sum(flat * flat, axis=1), 'core')]
  transfers between devices with their start and end apart: 5 -> 4, of which waited for: 4 -> 3; matrix products, arithmetic and copies ran while one was open for 2% -> 2% of each run, Pallas kernels for 0% -> 0%
where the time goes in v4:
time: 74.6 us; the launch traced here: 74.2 us
  waiting for transfers between devices  36.8 us (49%)
  blocking collectives  15.7 us (21%)
  starting transfers between devices  11.8 us (16%)
  other arithmetic  3.65 us (5%)
  local copies, waits for them, and re-layouts  3.58 us (5%)
  matrix products  2.43 us (3%)
    ppermute x4, waiting for transfers between devices, shifted(): return lax.ppermute(value, axis, pairs)  36.8 us
    ppermute x4, starting transfers between devices, shifted(): return lax.ppermute(value, axis, pairs)  11.8 us
    psum x1, blocking collectives, shards(): lax.psum(lax.psum(jnp.sum(flat * flat, axis=1), 'core'), 'chip')  8.57 us
    psum x1, blocking collectives, shards(): lax.psum(jnp.sum(flat * flat, axis=1), 'core')  7.11 us
    unnamed x14, local copies, waits for them, and re-layouts  2.05 us
  transfers between devices with their start and end apart: 4, of which 3 were waited for; matrix products, arithmetic and copies ran while one was open for 2% of the time, Pallas kernels for 0%

profile of v4, /device:TPU:1, one launch (start us, length us, event | category | flops | bytes accessed | tf_op | source)
XLA Modules:
  0.0 74.2 jit_solution(5578988756742886573)
XLA Ops:
  0.0 0.0 copy-start
  0.1 0.0 copy-start.6
  0.1 0.7 copy-done.6
  0.8 0.0 copy-start.5
  0.8 0.7 copy-done.5
  1.4 0.3 reduce-window.9
  1.7 0.1 slice.29
  1.9 0.1 slice_reduce_fusion
  2.0 0.0 copy-start.1
  2.0 0.0 copy-start.2
  2.0 1.1 %copy.37 = bf16[256,512]{0,1:T(8,128)(2,1)S(1)} copy(bf16[256,512]{1,0:T(8,128)(2,1)} %param.9) | data formatting | bytes 524288 | tf_op jit(solution)/shard_map/reshape | solution.py:56
  3.1 0.0 copy-start.4
  3.2 0.7 copy-done.4
  3.8 0.1 select_reduce_fusion
  4.0 0.7 fusion.31
  4.7 0.2 convert_reduce_fusion
  4.8 0.2 convert_reduce_fusion.2
  5.1 0.1 exponential_select_fusion.3
  5.2 0.7 broadcast_compare_fusion.1
  5.9 0.1 exponential_select_fusion.2
  5.9 0.0 copy-done.1
  6.0 0.0 copy-done.2
  6.0 0.4 convolution_add_fusion
  6.4 5.7 %collective-permute-start.1 = (f32[4,128,128]{2,1,0:T(8,128)S(1)}, f32[4,128,128]{2,1,0:T(8,128)S(1)}, u32[]{:S(2)}, u32[]{:S(2)}) collective-permute-start(f32[4,128,128]{2,1,0:T(8,128)S(1)} %convolution_add_fusion), channel_id=1, source_target_pairs={{0,16},{8,24},{16,32},{24,40},{32,48},{40,56},{48,64},{56,72},{64,... | collective-permute-start | bytes 786440 | tf_op jit(solution)/shard_map/ppermute | solution.py:11
  12.0 2.3 %collective-permute-start = (f32[4,128,128]{2,1,0:T(8,128)S(1)}, f32[4,128,128]{2,1,0:T(8,128)S(1)}, u32[]{:S(2)}, u32[]{:S(2)}) collective-permute-start(f32[4,128,128]{2,1,0:T(8,128)S(1)} %convolution_add_fusion), channel_id=1, source_target_pairs={{0,8},{8,16},{16,24},{24,32},{32,40},{40,48},{48,56},{56,64},{64,7... | collective-permute-start | bytes 786440 | tf_op jit(solution)/shard_map/ppermute | solution.py:11
  14.4 0.1 fusion.7
  14.5 0.1 fusion.20
  14.6 0.0 copy-done
  14.6 0.4 fusion.4
  15.1 0.3 fusion
  15.4 22.4 %collective-permute-done.1 = f32[4,128,128]{2,1,0:T(8,128)S(1)} collective-permute-done((f32[4,128,128]{2,1,0:T(8,128)S(1)}, f32[4,128,128]{2,1,0:T(8,128)S(1)}, u32[]{:S(2)}, u32[]{:S(2)}) %collective-permute-start.1) | collective-permute-done | bytes 262176 | tf_op jit(solution)/shard_map/ppermute | solution.py:11
  37.9 1.7 %collective-permute-done = f32[4,128,128]{2,1,0:T(8,128)S(1)} collective-permute-done((f32[4,128,128]{2,1,0:T(8,128)S(1)}, f32[4,128,128]{2,1,0:T(8,128)S(1)}, u32[]{:S(2)}, u32[]{:S(2)}) %collective-permute-start) | collective-permute-done | bytes 262176 | tf_op jit(solution)/shard_map/ppermute | solution.py:11
  39.5 0.1 multiply_add_fusion
  39.7 1.9 %collective-permute-start.3 = (f32[4,128,128]{2,1,0:T(8,128)S(1)}, f32[4,128,128]{2,1,0:T(8,128)S(1)}, u32[]{:S(2)}, u32[]{:S(2)}) collective-permute-start(f32[4,128,128]{2,1,0:T(8,128)S(1)} %multiply_add_fusion), channel_id=1, source_target_pairs={{0,48},{8,56},{16,64},{24,72},{32,80},{40,88},{48,96},{56,104},{64... | collective-permute-start | bytes 786440 | tf_op jit(solution)/shard_map/ppermute | solution.py:11
  41.6 1.9 %collective-permute-start.2 = (f32[4,128,128]{2,1,0:T(8,128)S(1)}, f32[4,128,128]{2,1,0:T(8,128)S(1)}, u32[]{:S(2)}, u32[]{:S(2)}) collective-permute-start(f32[4,128,128]{2,1,0:T(8,128)S(1)} %multiply_add_fusion), channel_id=1, source_target_pairs={{0,24},{8,32},{16,40},{24,48},{32,56},{40,64},{48,72},{56,80},{64,... | collective-permute-start | bytes 786440 | tf_op jit(solution)/shard_map/ppermute | solution.py:11
  43.5 0.7 convolution_bitcast_fusion.2
  44.2 12.7 %collective-permute-done.3 = f32[4,128,128]{2,1,0:T(8,128)S(1)} collective-permute-done((f32[4,128,128]{2,1,0:T(8,128)S(1)}, f32[4,128,128]{2,1,0:T(8,128)S(1)}, u32[]{:S(2)}, u32[]{:S(2)}) %collective-permute-start.3) | collective-permute-done | bytes 262176 | tf_op jit(solution)/shard_map/ppermute | solution.py:11
  57.0 0.0 collective-permute-done.2
  57.0 0.6 multiply_reduce_fusion
  57.5 0.2 copy.34
  57.7 7.1 %psum.14 = f32[256]{0:T(256)S(1)} all-reduce(f32[256]{0:T(256)S(1)} %get-tuple-element.27), channel_id=1, replica_groups=mesh['ctx'=128,'chip'=4,'core'=2] {'core'}, use_global_device_ids=true, to_apply=%region_8.9 | all-reduce | flops 256 | bytes 2048 | tf_op jit(solution)/shard_map/psum | solution.py:106
  64.8 0.0 copy-start.3
  64.8 8.6 %psum.15 = f32[256]{0:T(256)S(1)} all-reduce(f32[256]{0:T(256)S(1)} %psum.14), channel_id=1, replica_groups=mesh['ctx'=128,'chip'=4,'core'=2] {'chip'}, use_global_device_ids=true, to_apply=%region_9.10 | all-reduce | flops 256 | bytes 2048 | tf_op jit(solution)/shard_map/psum | solution.py:106
  73.4 0.0 copy-done.3
  73.4 0.8 %multiply_convert_fusion = bf16[256,512]{1,0:T(8,128)(2,1)} fusion(f32[256,512]{1,0:T(8,128)S(1)} %copy.34, f32[512]{0:T(512)S(1)} %copy-done.3, f32[256]{0:T(256)S(1)} %add_rsqrt_fusion), kind=kLoop, calls=%fused_computation.10 | loop fusion | flops 393216 | bytes 789504 | tf_op jit(solution)/shard_map/convert_element_type | solution.py:108
  (10 shorter events, 0.1 us)
Async XLA Ops:
  0.0 14.6 %copy-start = (bf16[256,512]{1,0:T(8,128)(2,1)S(1)}, bf16[256,512]{1,0:T(8,128)(2,1)}, u32[]{:S(2)}) copy-start(bf16[256,512]{1,0:T(8,128)(2,1)} %param.8) | copy-start | bytes 786436
  0.1 0.7 copy-start.6
  0.8 0.7 copy-start.5
  2.0 4.0 %copy-start.1 = (bf16[256,512]{1,0:T(8,128)(2,1)S(1)}, bf16[256,512]{1,0:T(8,128)(2,1)}, u32[]{:S(2)}) copy-start(bf16[256,512]{1,0:T(8,128)(2,1)} %param.10) | copy-start | bytes 786436
  2.0 4.0 %copy-start.2 = (f32[4,128,128]{2,1,0:T(8,128)S(1)}, f32[4,128,128]{2,1,0:T(8,128)}, u32[]{:S(2)}) copy-start(f32[4,128,128]{2,1,0:T(8,128)} %param.11) | copy-start | bytes 786436
  3.1 0.7 copy-start.4
  6.4 31.5 %collective-permute-start.1 = (f32[4,128,128]{2,1,0:T(8,128)S(1)}, f32[4,128,128]{2,1,0:T(8,128)S(1)}, u32[]{:S(2)}, u32[]{:S(2)}) collective-permute-start(f32[4,128,128]{2,1,0:T(8,128)S(1)} %convolution_add_fusion), channel_id=1, source_target_pairs={{0,16},{8,24},{16,32},{24,40},{32,48},{40,56},{48,64},{56,72},{64,... | collective-permute-start | bytes 786440 | tf_op jit(solution)/shard_map/ppermute | solution.py:11
  12.0 27.5 %collective-permute-start = (f32[4,128,128]{2,1,0:T(8,128)S(1)}, f32[4,128,128]{2,1,0:T(8,128)S(1)}, u32[]{:S(2)}, u32[]{:S(2)}) collective-permute-start(f32[4,128,128]{2,1,0:T(8,128)S(1)} %convolution_add_fusion), channel_id=1, source_target_pairs={{0,8},{8,16},{16,24},{24,32},{32,40},{40,48},{48,56},{56,64},{64,7... | collective-permute-start | bytes 786440 | tf_op jit(solution)/shard_map/ppermute | solution.py:11
  39.7 17.3 %collective-permute-start.3 = (f32[4,128,128]{2,1,0:T(8,128)S(1)}, f32[4,128,128]{2,1,0:T(8,128)S(1)}, u32[]{:S(2)}, u32[]{:S(2)}) collective-permute-start(f32[4,128,128]{2,1,0:T(8,128)S(1)} %multiply_add_fusion), channel_id=1, source_target_pairs={{0,48},{8,56},{16,64},{24,72},{32,80},{40,88},{48,96},{56,104},{64... | collective-permute-start | bytes 786440 | tf_op jit(solution)/shard_map/ppermute | solution.py:11
  41.6 15.4 %collective-permute-start.2 = (f32[4,128,128]{2,1,0:T(8,128)S(1)}, f32[4,128,128]{2,1,0:T(8,128)S(1)}, u32[]{:S(2)}, u32[]{:S(2)}) collective-permute-start(f32[4,128,128]{2,1,0:T(8,128)S(1)} %multiply_add_fusion), channel_id=1, source_target_pairs={{0,24},{8,32},{16,40},{24,48},{32,56},{40,64},{48,72},{56,80},{64,... | collective-permute-start | bytes 786440 | tf_op jit(solution)/shard_map/ppermute | solution.py:11
  64.8 8.6 %copy-start.3 = (f32[512]{0:T(512)S(1)}, f32[512]{0:T(512)}, u32[]{:S(2)}) copy-start(f32[512]{0:T(512)} %param.13) | copy-start | bytes 6148

commit v5 on v4

--- a/solution.py
+++ b/solution.py
@@ -103,7 +103,13 @@
     attn = attn + carried * lead_in[:, :, None] + started * lead_init[:, :, None]
 
     flat = attn.reshape(row_count, feature_count)
-    square_total = lax.psum(lax.psum(jnp.sum(flat * flat, axis=1), "core"), "chip")
+    on_chip = lax.psum(jnp.sum(flat * flat, axis=1), "core")
+    chips = lax.axis_size("chip")
+    square_total = on_chip
+    for step in range(1, chips):
+        square_total = square_total + lax.ppermute(
+            on_chip, "chip", [(source, (source + step) % chips) for source in range(chips)]
+        )
     mean_sq = square_total / jnp.float32(feature_count * lax.axis_size("chip") * lax.axis_size("core"))
     return (flat * lax.rsqrt(mean_sq + 1e-05)[:, None] * norm_gain[None, :]).astype(jnp.bfloat16)
 

time: 74.6 us -> 78.2 us (1.048)
  starting transfers between devices: 11.8 us -> 21.1 us
  blocking collectives: 15.7 us -> 7.11 us
  waiting for transfers between devices: 36.8 us -> 39.6 us
    ppermute x0 -> x3, starting transfers between devices: none -> 9.31 us  [shards(): lax.ppermute(on_chip, 'chip', [(source, (source + step) % chips) for sour...]
    psum x2 -> x1, blocking collectives: 15.7 us -> 7.11 us  [shards(): on_chip = lax.psum(jnp.sum(flat * flat, axis=1), 'core')]
    ppermute x0 -> x3, waiting for transfers between devices: none -> 2.78 us  [shards(): lax.ppermute(on_chip, 'chip', [(source, (source + step) % chips) for sour...]
  transfers between devices with their start and end apart: 4 -> 7, of which waited for: 3 -> 5; matrix products, arithmetic and copies ran while one was open for 2% -> 2% of each run, Pallas kernels for 0% -> 0%
where the time goes in v5:
time: 78.2 us; the launch traced here: 77.8 us
  waiting for transfers between devices  39.6 us (51%)
  starting transfers between devices  21.1 us (27%)
  blocking collectives  7.11 us (9%)
  other arithmetic  3.64 us (5%)
  local copies, waits for them, and re-layouts  3.59 us (5%)
  matrix products  2.43 us (3%)
    ppermute x4, waiting for transfers between devices, shifted(): return lax.ppermute(value, axis, pairs)  36.8 us
    ppermute x4, starting transfers between devices, shifted(): return lax.ppermute(value, axis, pairs)  11.8 us
    ppermute x3, starting transfers between devices, shards(): lax.ppermute(on_chip, 'chip', [(source, (source + step) % chips) for sour...  9.31 us
    psum x1, blocking collectives, shards(): on_chip = lax.psum(jnp.sum(flat * flat, axis=1), 'core')  7.11 us
    ppermute x3, waiting for transfers between devices, shards(): lax.ppermute(on_chip, 'chip', [(source, (source + step) % chips) for sour...  2.78 us
    unnamed x14, local copies, waits for them, and re-layouts  2.05 us
  transfers between devices with their start and end apart: 7, of which 5 were waited for; matrix products, arithmetic and copies ran while one was open for 2% of the time, Pallas kernels for 0%

profile of v5, /device:TPU:1, one launch (start us, length us, event | category | flops | bytes accessed | tf_op | source)
XLA Modules:
  0.0 77.8 jit_solution(93737473339129017)
XLA Ops:
  0.0 0.0 copy-start
  0.1 0.0 copy-start.6
  0.1 0.7 copy-done.6
  0.8 0.7 copy-done.5
  1.4 0.3 reduce-window.9
  1.7 0.1 slice.29
  1.9 0.1 slice_reduce_fusion
  2.0 0.0 copy-start.2
  2.0 1.1 %copy.37 = bf16[256,512]{0,1:T(8,128)(2,1)S(1)} copy(bf16[256,512]{1,0:T(8,128)(2,1)} %param.9) | data formatting | bytes 524288 | tf_op jit(solution)/shard_map/reshape | solution.py:56
  3.1 0.0 copy-start.4
  3.2 0.7 copy-done.4
  3.8 0.1 select_reduce_fusion
  4.0 0.7 fusion.31
  4.7 0.2 convert_reduce_fusion
  4.8 0.2 convert_reduce_fusion.2
  5.1 0.1 exponential_select_fusion.3
  5.2 0.7 broadcast_compare_fusion.1
  5.9 0.1 exponential_select_fusion.2
  5.9 0.0 copy-done.1
  6.0 0.0 copy-done.2
  6.0 0.4 convolution_add_fusion
  6.4 5.7 %collective-permute-start.1 = (f32[4,128,128]{2,1,0:T(8,128)S(1)}, f32[4,128,128]{2,1,0:T(8,128)S(1)}, u32[]{:S(2)}, u32[]{:S(2)}) collective-permute-start(f32[4,128,128]{2,1,0:T(8,128)S(1)} %convolution_add_fusion), channel_id=1, source_target_pairs={{0,16},{8,24},{16,32},{24,40},{32,48},{40,56},{48,64},{56,72},{64,... | collective-permute-start | bytes 786440 | tf_op jit(solution)/shard_map/ppermute | solution.py:11
  12.0 2.3 %collective-permute-start = (f32[4,128,128]{2,1,0:T(8,128)S(1)}, f32[4,128,128]{2,1,0:T(8,128)S(1)}, u32[]{:S(2)}, u32[]{:S(2)}) collective-permute-start(f32[4,128,128]{2,1,0:T(8,128)S(1)} %convolution_add_fusion), channel_id=1, source_target_pairs={{0,8},{8,16},{16,24},{24,32},{32,40},{40,48},{48,56},{56,64},{64,7... | collective-permute-start | bytes 786440 | tf_op jit(solution)/shard_map/ppermute | solution.py:11
  14.4 0.1 fusion.7
  14.5 0.1 fusion.20
  14.6 0.0 copy-done
  14.6 0.4 fusion.4
  15.1 0.3 fusion
  15.4 22.4 %collective-permute-done.1 = f32[4,128,128]{2,1,0:T(8,128)S(1)} collective-permute-done((f32[4,128,128]{2,1,0:T(8,128)S(1)}, f32[4,128,128]{2,1,0:T(8,128)S(1)}, u32[]{:S(2)}, u32[]{:S(2)}) %collective-permute-start.1) | collective-permute-done | bytes 262176 | tf_op jit(solution)/shard_map/ppermute | solution.py:11
  37.9 1.7 %collective-permute-done = f32[4,128,128]{2,1,0:T(8,128)S(1)} collective-permute-done((f32[4,128,128]{2,1,0:T(8,128)S(1)}, f32[4,128,128]{2,1,0:T(8,128)S(1)}, u32[]{:S(2)}, u32[]{:S(2)}) %collective-permute-start) | collective-permute-done | bytes 262176 | tf_op jit(solution)/shard_map/ppermute | solution.py:11
  39.5 0.1 multiply_add_fusion
  39.7 1.9 %collective-permute-start.3 = (f32[4,128,128]{2,1,0:T(8,128)S(1)}, f32[4,128,128]{2,1,0:T(8,128)S(1)}, u32[]{:S(2)}, u32[]{:S(2)}) collective-permute-start(f32[4,128,128]{2,1,0:T(8,128)S(1)} %multiply_add_fusion), channel_id=1, source_target_pairs={{0,48},{8,56},{16,64},{24,72},{32,80},{40,88},{48,96},{56,104},{64... | collective-permute-start | bytes 786440 | tf_op jit(solution)/shard_map/ppermute | solution.py:11
  41.6 1.9 %collective-permute-start.2 = (f32[4,128,128]{2,1,0:T(8,128)S(1)}, f32[4,128,128]{2,1,0:T(8,128)S(1)}, u32[]{:S(2)}, u32[]{:S(2)}) collective-permute-start(f32[4,128,128]{2,1,0:T(8,128)S(1)} %multiply_add_fusion), channel_id=1, source_target_pairs={{0,24},{8,32},{16,40},{24,48},{32,56},{40,64},{48,72},{56,80},{64,... | collective-permute-start | bytes 786440 | tf_op jit(solution)/shard_map/ppermute | solution.py:11
  43.5 0.7 convolution_bitcast_fusion.2
  44.2 12.7 %collective-permute-done.3 = f32[4,128,128]{2,1,0:T(8,128)S(1)} collective-permute-done((f32[4,128,128]{2,1,0:T(8,128)S(1)}, f32[4,128,128]{2,1,0:T(8,128)S(1)}, u32[]{:S(2)}, u32[]{:S(2)}) %collective-permute-start.3) | collective-permute-done | bytes 262176 | tf_op jit(solution)/shard_map/ppermute | solution.py:11
  57.0 0.0 collective-permute-done.2
  57.0 0.6 multiply_reduce_fusion
  57.5 7.1 %psum.7 = f32[256]{0:T(256)S(1)} all-reduce(f32[256]{0:T(256)S(1)} %get-tuple-element.27), channel_id=1, replica_groups=mesh['ctx'=128,'chip'=4,'core'=2] {'core'}, use_global_device_ids=true, to_apply=%region_8.9 | all-reduce | flops 256 | bytes 2048 | tf_op jit(solution)/shard_map/psum | solution.py:106
  64.6 4.4 %collective-permute-start.6 = (f32[256]{0:T(256)S(1)}, f32[256]{0:T(256)S(1)}, u32[]{:S(2)}, u32[]{:S(2)}) collective-permute-start(f32[256]{0:T(256)S(1)} %psum.7), channel_id=1, source_target_pairs={{0,6},{2,0},{4,2},{6,4},{1,7},{3,1},{5,3},{7,5},{8,14},{10,8},{12,... | collective-permute-start | bytes 3080 | tf_op jit(solution)/shard_map/ppermute | solution.py:110
  69.0 2.4 %collective-permute-start.5 = (f32[256]{0:T(256)S(1)}, f32[256]{0:T(256)S(1)}, u32[]{:S(2)}, u32[]{:S(2)}) collective-permute-start(f32[256]{0:T(256)S(1)} %psum.7), channel_id=1, source_target_pairs={{0,4},{2,6},{4,0},{6,2},{1,5},{3,7},{5,1},{7,3},{8,12},{10,14},{12... | collective-permute-start | bytes 3080 | tf_op jit(solution)/shard_map/ppermute | solution.py:110
  71.4 2.5 %collective-permute-start.4 = (f32[256]{0:T(256)S(1)}, f32[256]{0:T(256)S(1)}, u32[]{:S(2)}, u32[]{:S(2)}) collective-permute-start(f32[256]{0:T(256)S(1)} %psum.7), channel_id=1, source_target_pairs={{0,2},{2,4},{4,6},{6,0},{1,3},{3,5},{5,7},{7,1},{8,10},{10,12},{12... | collective-permute-start | bytes 3080 | tf_op jit(solution)/shard_map/ppermute | solution.py:110
  74.0 0.2 copy.34
  74.2 0.0 copy-start.3
  74.2 0.0 collective-permute-done.6
  74.2 0.6 collective-permute-done.5
  74.8 2.1 %collective-permute-done.4 = f32[256]{0:T(256)S(1)} collective-permute-done((f32[256]{0:T(256)S(1)}, f32[256]{0:T(256)S(1)}, u32[]{:S(2)}, u32[]{:S(2)}) %collective-permute-start.4) | collective-permute-done | bytes 1056 | tf_op jit(solution)/shard_map/ppermute | solution.py:110
  77.0 0.0 copy-done.3
  77.0 0.8 %multiply_convert_fusion = bf16[256,512]{1,0:T(8,128)(2,1)} fusion(f32[256,512]{1,0:T(8,128)S(1)} %copy.34, f32[512]{0:T(512)S(1)} %copy-done.3, f32[256]{0:T(256)S(1)} %add_rsqrt_fusion), kind=kLoop, calls=%fused_computation.10 | loop fusion | flops 393216 | bytes 789504 | tf_op jit(solution)/shard_map/convert_element_type | solution.py:114
  (12 shorter events, 0.1 us)
Async XLA Ops:
  0.0 14.6 %copy-start = (bf16[256,512]{1,0:T(8,128)(2,1)S(1)}, bf16[256,512]{1,0:T(8,128)(2,1)}, u32[]{:S(2)}) copy-start(bf16[256,512]{1,0:T(8,128)(2,1)} %param.8) | copy-start | bytes 786436
  0.1 0.7 copy-start.6
  0.8 0.7 copy-start.5
  2.0 4.0 %copy-start.1 = (bf16[256,512]{1,0:T(8,128)(2,1)S(1)}, bf16[256,512]{1,0:T(8,128)(2,1)}, u32[]{:S(2)}) copy-start(bf16[256,512]{1,0:T(8,128)(2,1)} %param.10) | copy-start | bytes 786436
  2.0 4.0 %copy-start.2 = (f32[4,128,128]{2,1,0:T(8,128)S(1)}, f32[4,128,128]{2,1,0:T(8,128)}, u32[]{:S(2)}) copy-start(f32[4,128,128]{2,1,0:T(8,128)} %param.11) | copy-start | bytes 786436
  3.1 0.7 copy-start.4
  6.4 31.5 %collective-permute-start.1 = (f32[4,128,128]{2,1,0:T(8,128)S(1)}, f32[4,128,128]{2,1,0:T(8,128)S(1)}, u32[]{:S(2)}, u32[]{:S(2)}) collective-permute-start(f32[4,128,128]{2,1,0:T(8,128)S(1)} %convolution_add_fusion), channel_id=1, source_target_pairs={{0,16},{8,24},{16,32},{24,40},{32,48},{40,56},{48,64},{56,72},{64,... | collective-permute-start | bytes 786440 | tf_op jit(solution)/shard_map/ppermute | solution.py:11
  12.0 27.5 %collective-permute-start = (f32[4,128,128]{2,1,0:T(8,128)S(1)}, f32[4,128,128]{2,1,0:T(8,128)S(1)}, u32[]{:S(2)}, u32[]{:S(2)}) collective-permute-start(f32[4,128,128]{2,1,0:T(8,128)S(1)} %convolution_add_fusion), channel_id=1, source_target_pairs={{0,8},{8,16},{16,24},{24,32},{32,40},{40,48},{48,56},{56,64},{64,7... | collective-permute-start | bytes 786440 | tf_op jit(solution)/shard_map/ppermute | solution.py:11
  39.7 17.3 %collective-permute-start.3 = (f32[4,128,128]{2,1,0:T(8,128)S(1)}, f32[4,128,128]{2,1,0:T(8,128)S(1)}, u32[]{:S(2)}, u32[]{:S(2)}) collective-permute-start(f32[4,128,128]{2,1,0:T(8,128)S(1)} %multiply_add_fusion), channel_id=1, source_target_pairs={{0,48},{8,56},{16,64},{24,72},{32,80},{40,88},{48,96},{56,104},{64... | collective-permute-start | bytes 786440 | tf_op jit(solution)/shard_map/ppermute | solution.py:11
  41.6 15.4 %collective-permute-start.2 = (f32[4,128,128]{2,1,0:T(8,128)S(1)}, f32[4,128,128]{2,1,0:T(8,128)S(1)}, u32[]{:S(2)}, u32[]{:S(2)}) collective-permute-start(f32[4,128,128]{2,1,0:T(8,128)S(1)} %multiply_add_fusion), channel_id=1, source_target_pairs={{0,24},{8,32},{16,40},{24,48},{32,56},{40,64},{48,72},{56,80},{64,... | collective-permute-start | bytes 786440 | tf_op jit(solution)/shard_map/ppermute | solution.py:11
  64.6 9.6 %collective-permute-start.6 = (f32[256]{0:T(256)S(1)}, f32[256]{0:T(256)S(1)}, u32[]{:S(2)}, u32[]{:S(2)}) collective-permute-start(f32[256]{0:T(256)S(1)} %psum.7), channel_id=1, source_target_pairs={{0,6},{2,0},{4,2},{6,4},{1,7},{3,1},{5,3},{7,5},{8,14},{10,8},{12,... | collective-permute-start | bytes 3080 | tf_op jit(solution)/shard_map/ppermute | solution.py:110
  69.0 5.8 %collective-permute-start.5 = (f32[256]{0:T(256)S(1)}, f32[256]{0:T(256)S(1)}, u32[]{:S(2)}, u32[]{:S(2)}) collective-permute-start(f32[256]{0:T(256)S(1)} %psum.7), channel_id=1, source_target_pairs={{0,4},{2,6},{4,0},{6,2},{1,5},{3,7},{5,1},{7,3},{8,12},{10,14},{12... | collective-permute-start | bytes 3080 | tf_op jit(solution)/shard_map/ppermute | solution.py:110
  71.4 5.5 %collective-permute-start.4 = (f32[256]{0:T(256)S(1)}, f32[256]{0:T(256)S(1)}, u32[]{:S(2)}, u32[]{:S(2)}) collective-permute-start(f32[256]{0:T(256)S(1)} %psum.7), channel_id=1, source_target_pairs={{0,2},{2,4},{4,6},{6,0},{1,3},{3,5},{5,7},{7,1},{8,10},{10,12},{12... | collective-permute-start | bytes 3080 | tf_op jit(solution)/shard_map/ppermute | solution.py:110
  74.2 2.8 %copy-start.3 = (f32[512]{0:T(512)S(1)}, f32[512]{0:T(512)}, u32[]{:S(2)}) copy-start(f32[512]{0:T(512)} %param.13) | copy-start | bytes 6148

commit v6 on v4

--- a/solution.py
+++ b/solution.py
@@ -103,7 +103,9 @@
     attn = attn + carried * lead_in[:, :, None] + started * lead_init[:, :, None]
 
     flat = attn.reshape(row_count, feature_count)
-    square_total = lax.psum(lax.psum(jnp.sum(flat * flat, axis=1), "core"), "chip")
+    groups = lax.axis_size("chip") * lax.axis_size("core")
+    part = jnp.broadcast_to(jnp.sum(flat * flat, axis=1)[None], (groups, row_count))
+    square_total = jnp.sum(lax.all_to_all(part, ("chip", "core"), 0, 0), axis=0)
     mean_sq = square_total / jnp.float32(feature_count * lax.axis_size("chip") * lax.axis_size("core"))
     return (flat * lax.rsqrt(mean_sq + 1e-05)[:, None] * norm_gain[None, :]).astype(jnp.bfloat16)
 

time: 74.6 us -> 73.9 us (level)
  blocking collectives: 15.7 us -> 0 us
  starting transfers between devices: 11.8 us -> 21.1 us
  waiting for transfers between devices: 36.8 us -> 41.3 us
  local copies, waits for them, and re-layouts: 3.58 us -> 4.86 us
    psum x2 -> x0, blocking collectives: 15.7 us -> none  [the longest x1 8.57 us: shards(): lax.psum(lax.psum(jnp.sum(flat * flat, axis=1), 'core'), 'chip')]
    all_to_all x0 -> x1, starting transfers between devices: none -> 9.28 us  [shards(): square_total = jnp.sum(lax.all_to_all(part, ('chip', 'core'), 0, 0), axis=0)]
    all_to_all x0 -> x1, waiting for transfers between devices: none -> 4.41 us  [shards(): square_total = jnp.sum(lax.all_to_all(part, ('chip', 'core'), 0, 0), axis=0)]
  transfers between devices with their start and end apart: 4 -> 5, of which waited for: 3 -> 4; matrix products, arithmetic and copies ran while one was open for 2% -> 3% of each run, Pallas kernels for 0% -> 0%
where the time goes in v6:
time: 73.9 us; the launch traced here: 73.5 us
  waiting for transfers between devices  41.3 us (56%)
  starting transfers between devices  21.1 us (29%)
  local copies, waits for them, and re-layouts  4.86 us (7%)
  other arithmetic  3.66 us (5%)
  matrix products  2.43 us (3%)
    ppermute x4, waiting for transfers between devices, shifted(): return lax.ppermute(value, axis, pairs)  36.8 us
    ppermute x4, starting transfers between devices, shifted(): return lax.ppermute(value, axis, pairs)  11.8 us
    all_to_all x1, starting transfers between devices, shards(): square_total = jnp.sum(lax.all_to_all(part, ('chip', 'core'), 0, 0), axis=0)  9.28 us
    all_to_all x1, waiting for transfers between devices, shards(): square_total = jnp.sum(lax.all_to_all(part, ('chip', 'core'), 0, 0), axis=0)  4.41 us
    unnamed x14, local copies, waits for them, and re-layouts  2.72 us
  transfers between devices with their start and end apart: 5, of which 4 were waited for; matrix products, arithmetic and copies ran while one was open for 3% of the time, Pallas kernels for 0%

profile of v6, /device:TPU:1, one launch (start us, length us, event | category | flops | bytes accessed | tf_op | source)
XLA Modules:
  0.0 73.5 jit_solution(10626502016241341913)
XLA Ops:
  0.0 0.0 copy-start
  0.1 0.0 copy-start.6
  0.1 0.7 copy-done.6
  0.8 0.0 copy-start.5
  0.8 0.7 copy-done.5
  1.4 0.3 reduce-window.9
  1.7 0.1 slice.29
  1.9 0.1 slice_reduce_fusion
  2.0 0.0 copy-start.1
  2.0 0.0 copy-start.2
  2.0 1.1 %copy.49 = bf16[256,512]{0,1:T(8,128)(2,1)S(1)} copy(bf16[256,512]{1,0:T(8,128)(2,1)} %param.9) | data formatting | bytes 524288 | tf_op jit(solution)/shard_map/reshape | solution.py:56
  3.1 0.0 copy-start.4
  3.2 0.7 copy-done.4
  3.8 0.1 select_reduce_fusion
  4.0 0.7 fusion.31
  4.7 0.2 convert_reduce_fusion
  4.8 0.2 convert_reduce_fusion.2
  5.1 0.1 exponential_select_fusion.3
  5.2 0.7 broadcast_compare_fusion.1
  5.9 0.1 exponential_select_fusion.2
  5.9 0.0 copy-done.1
  6.0 0.0 copy-done.2
  6.0 0.4 convolution_add_fusion
  6.4 5.7 %collective-permute-start.1 = (f32[4,128,128]{2,1,0:T(8,128)S(1)}, f32[4,128,128]{2,1,0:T(8,128)S(1)}, u32[]{:S(2)}, u32[]{:S(2)}) collective-permute-start(f32[4,128,128]{2,1,0:T(8,128)S(1)} %convolution_add_fusion), channel_id=1, source_target_pairs={{0,16},{8,24},{16,32},{24,40},{32,48},{40,56},{48,64},{56,72},{64,... | collective-permute-start | bytes 786440 | tf_op jit(solution)/shard_map/ppermute | solution.py:11
  12.0 2.3 %collective-permute-start = (f32[4,128,128]{2,1,0:T(8,128)S(1)}, f32[4,128,128]{2,1,0:T(8,128)S(1)}, u32[]{:S(2)}, u32[]{:S(2)}) collective-permute-start(f32[4,128,128]{2,1,0:T(8,128)S(1)} %convolution_add_fusion), channel_id=1, source_target_pairs={{0,8},{8,16},{16,24},{24,32},{32,40},{40,48},{48,56},{56,64},{64,7... | collective-permute-start | bytes 786440 | tf_op jit(solution)/shard_map/ppermute | solution.py:11
  14.4 0.1 fusion.7
  14.5 0.1 fusion.20
  14.6 0.0 copy-done
  14.6 0.4 fusion.4
  15.1 0.3 fusion
  15.4 22.4 %collective-permute-done.1 = f32[4,128,128]{2,1,0:T(8,128)S(1)} collective-permute-done((f32[4,128,128]{2,1,0:T(8,128)S(1)}, f32[4,128,128]{2,1,0:T(8,128)S(1)}, u32[]{:S(2)}, u32[]{:S(2)}) %collective-permute-start.1) | collective-permute-done | bytes 262176 | tf_op jit(solution)/shard_map/ppermute | solution.py:11
  37.9 1.7 %collective-permute-done = f32[4,128,128]{2,1,0:T(8,128)S(1)} collective-permute-done((f32[4,128,128]{2,1,0:T(8,128)S(1)}, f32[4,128,128]{2,1,0:T(8,128)S(1)}, u32[]{:S(2)}, u32[]{:S(2)}) %collective-permute-start) | collective-permute-done | bytes 262176 | tf_op jit(solution)/shard_map/ppermute | solution.py:11
  39.5 0.1 multiply_add_fusion
  39.7 1.9 %collective-permute-start.3 = (f32[4,128,128]{2,1,0:T(8,128)S(1)}, f32[4,128,128]{2,1,0:T(8,128)S(1)}, u32[]{:S(2)}, u32[]{:S(2)}) collective-permute-start(f32[4,128,128]{2,1,0:T(8,128)S(1)} %multiply_add_fusion), channel_id=1, source_target_pairs={{0,48},{8,56},{16,64},{24,72},{32,80},{40,88},{48,96},{56,104},{64... | collective-permute-start | bytes 786440 | tf_op jit(solution)/shard_map/ppermute | solution.py:11
  41.6 1.9 %collective-permute-start.2 = (f32[4,128,128]{2,1,0:T(8,128)S(1)}, f32[4,128,128]{2,1,0:T(8,128)S(1)}, u32[]{:S(2)}, u32[]{:S(2)}) collective-permute-start(f32[4,128,128]{2,1,0:T(8,128)S(1)} %multiply_add_fusion), channel_id=1, source_target_pairs={{0,24},{8,32},{16,40},{24,48},{32,56},{40,64},{48,72},{56,80},{64,... | collective-permute-start | bytes 786440 | tf_op jit(solution)/shard_map/ppermute | solution.py:11
  43.5 0.7 convolution_bitcast_fusion.2
  44.2 12.7 %collective-permute-done.3 = f32[4,128,128]{2,1,0:T(8,128)S(1)} collective-permute-done((f32[4,128,128]{2,1,0:T(8,128)S(1)}, f32[4,128,128]{2,1,0:T(8,128)S(1)}, u32[]{:S(2)}, u32[]{:S(2)}) %collective-permute-start.3) | collective-permute-done | bytes 262176 | tf_op jit(solution)/shard_map/ppermute | solution.py:11
  57.0 0.0 collective-permute-done.2
  57.0 0.6 multiply_reduce_fusion
  57.5 0.6 broadcast_in_dim.118
  58.1 9.3 %all-to-all-start = ((f32[8,1,256]{2,1,0:T(1,128)}), f32[8,1,256]{2,1,0:T(1,128)S(1)}, u32[]{:S(2)}, u32[]{:S(2)}) async-start(f32[8,1,256]{2,1,0:T(1,128)} %broadcast_in_dim.118), calls=%async_computation | async-start | bytes 16384 | tf_op jit(solution)/shard_map/all_to_all | solution.py:108
  67.4 0.2 copy.45
  67.6 4.4 %all-to-all-done = f32[8,1,256]{2,1,0:T(1,128)S(1)} async-done(((f32[8,1,256]{2,1,0:T(1,128)}), f32[8,1,256]{2,1,0:T(1,128)S(1)}, u32[]{:S(2)}, u32[]{:S(2)}) %all-to-all-start) | async-done | bytes 8224 | tf_op jit(solution)/shard_map/all_to_all | solution.py:108
  72.0 0.0 copy-start.3
  72.1 0.7 copy-done.3
  72.7 0.8 %multiply_convert_fusion = bf16[256,512]{1,0:T(8,128)(2,1)} fusion(f32[256,512]{1,0:T(8,128)S(1)} %copy.45, f32[512]{0:T(512)S(1)} %copy-done.3, f32[256]{0:T(256)S(1)} %add_rsqrt_fusion), kind=kLoop, calls=%fused_computation.10 | loop fusion | flops 393216 | bytes 789504 | tf_op jit(solution)/shard_map/convert_element_type | solution.py:110
  (11 shorter events, 0.1 us)
Async XLA Ops:
  0.0 14.6 %copy-start = (bf16[256,512]{1,0:T(8,128)(2,1)S(1)}, bf16[256,512]{1,0:T(8,128)(2,1)}, u32[]{:S(2)}) copy-start(bf16[256,512]{1,0:T(8,128)(2,1)} %param.8) | copy-start | bytes 786436
  0.1 0.7 copy-start.6
  0.8 0.7 copy-start.5
  2.0 4.0 %copy-start.1 = (bf16[256,512]{1,0:T(8,128)(2,1)S(1)}, bf16[256,512]{1,0:T(8,128)(2,1)}, u32[]{:S(2)}) copy-start(bf16[256,512]{1,0:T(8,128)(2,1)} %param.10) | copy-start | bytes 786436
  2.0 4.0 %copy-start.2 = (f32[4,128,128]{2,1,0:T(8,128)S(1)}, f32[4,128,128]{2,1,0:T(8,128)}, u32[]{:S(2)}) copy-start(f32[4,128,128]{2,1,0:T(8,128)} %param.11) | copy-start | bytes 786436
  3.1 0.7 copy-start.4
  6.4 31.5 %collective-permute-start.1 = (f32[4,128,128]{2,1,0:T(8,128)S(1)}, f32[4,128,128]{2,1,0:T(8,128)S(1)}, u32[]{:S(2)}, u32[]{:S(2)}) collective-permute-start(f32[4,128,128]{2,1,0:T(8,128)S(1)} %convolution_add_fusion), channel_id=1, source_target_pairs={{0,16},{8,24},{16,32},{24,40},{32,48},{40,56},{48,64},{56,72},{64,... | collective-permute-start | bytes 786440 | tf_op jit(solution)/shard_map/ppermute | solution.py:11
  12.0 27.5 %collective-permute-start = (f32[4,128,128]{2,1,0:T(8,128)S(1)}, f32[4,128,128]{2,1,0:T(8,128)S(1)}, u32[]{:S(2)}, u32[]{:S(2)}) collective-permute-start(f32[4,128,128]{2,1,0:T(8,128)S(1)} %convolution_add_fusion), channel_id=1, source_target_pairs={{0,8},{8,16},{16,24},{24,32},{32,40},{40,48},{48,56},{56,64},{64,7... | collective-permute-start | bytes 786440 | tf_op jit(solution)/shard_map/ppermute | solution.py:11
  39.7 17.3 %collective-permute-start.3 = (f32[4,128,128]{2,1,0:T(8,128)S(1)}, f32[4,128,128]{2,1,0:T(8,128)S(1)}, u32[]{:S(2)}, u32[]{:S(2)}) collective-permute-start(f32[4,128,128]{2,1,0:T(8,128)S(1)} %multiply_add_fusion), channel_id=1, source_target_pairs={{0,48},{8,56},{16,64},{24,72},{32,80},{40,88},{48,96},{56,104},{64... | collective-permute-start | bytes 786440 | tf_op jit(solution)/shard_map/ppermute | solution.py:11
  41.6 15.4 %collective-permute-start.2 = (f32[4,128,128]{2,1,0:T(8,128)S(1)}, f32[4,128,128]{2,1,0:T(8,128)S(1)}, u32[]{:S(2)}, u32[]{:S(2)}) collective-permute-start(f32[4,128,128]{2,1,0:T(8,128)S(1)} %multiply_add_fusion), channel_id=1, source_target_pairs={{0,24},{8,32},{16,40},{24,48},{32,56},{40,64},{48,72},{56,80},{64,... | collective-permute-start | bytes 786440 | tf_op jit(solution)/shard_map/ppermute | solution.py:11
  58.1 13.9 %all-to-all-start = ((f32[8,1,256]{2,1,0:T(1,128)}), f32[8,1,256]{2,1,0:T(1,128)S(1)}, u32[]{:S(2)}, u32[]{:S(2)}) async-start(f32[8,1,256]{2,1,0:T(1,128)} %broadcast_in_dim.118), calls=%async_computation | async-start | bytes 16384 | tf_op jit(solution)/shard_map/all_to_all | solution.py:108
  72.0 0.7 copy-start.3

commit v7 on v3

--- a/solution.py
+++ b/solution.py
@@ -106,7 +106,9 @@
     attn = attn + carried * lead_in[:, :, None] + started * lead_init[:, :, None]
 
     flat = attn.reshape(row_count, feature_count)
-    square_total = lax.psum(lax.psum(jnp.sum(flat * flat, axis=1), "core"), "chip")
+    groups = lax.axis_size("chip") * lax.axis_size("core")
+    part = jnp.broadcast_to(jnp.sum(flat * flat, axis=1)[None], (groups, row_count))
+    square_total = jnp.sum(lax.all_to_all(part, ("chip", "core"), 0, 0), axis=0)
     mean_sq = square_total / jnp.float32(feature_count * lax.axis_size("chip") * lax.axis_size("core"))
     return (flat * lax.rsqrt(mean_sq + 1e-05)[:, None] * norm_gain[None, :]).astype(jnp.bfloat16)
 

time: 74.2 us -> 73.5 us (level)
  blocking collectives: 12.9 us -> 0 us
  starting transfers between devices: 17.2 us -> 23.7 us
  waiting for transfers between devices: 33.7 us -> 38.2 us
  local copies, waits for them, and re-layouts: 3.58 us -> 4.86 us
    psum x2 -> x0, blocking collectives: 12.9 us -> none  [the longest x1 8.57 us: shards(): lax.psum(lax.psum(jnp.sum(flat * flat, axis=1), 'core'), 'chip')]
    all_to_all x0 -> x1, starting transfers between devices: none -> 6.54 us  [shards(): square_total = jnp.sum(lax.all_to_all(part, ('chip', 'core'), 0, 0), axis=0)]
    all_to_all x0 -> x1, waiting for transfers between devices: none -> 4.41 us  [shards(): square_total = jnp.sum(lax.all_to_all(part, ('chip', 'core'), 0, 0), axis=0)]
  transfers between devices with their start and end apart: 5 -> 6, of which waited for: 4 -> 5; matrix products, arithmetic and copies ran while one was open for 2% -> 3% of each run, Pallas kernels for 0% -> 0%
where the time goes in v7:
time: 73.5 us; the launch traced here: 73.1 us
  waiting for transfers between devices  38.2 us (52%)
  starting transfers between devices  23.7 us (32%)
  local copies, waits for them, and re-layouts  4.86 us (7%)
  other arithmetic  3.7 us (5%)
  matrix products  2.43 us (3%)
    ppermute x5, waiting for transfers between devices, shifted(): return lax.ppermute(value, axis, pairs)  33.7 us
    ppermute x5, starting transfers between devices, shifted(): return lax.ppermute(value, axis, pairs)  17.2 us
    all_to_all x1, starting transfers between devices, shards(): square_total = jnp.sum(lax.all_to_all(part, ('chip', 'core'), 0, 0), axis=0)  6.54 us
    all_to_all x1, waiting for transfers between devices, shards(): square_total = jnp.sum(lax.all_to_all(part, ('chip', 'core'), 0, 0), axis=0)  4.41 us
    unnamed x14, local copies, waits for them, and re-layouts  2.72 us
  transfers between devices with their start and end apart: 6, of which 5 were waited for; matrix products, arithmetic and copies ran while one was open for 3% of the time, Pallas kernels for 0%

profile of v7, /device:TPU:1, one launch (start us, length us, event | category | flops | bytes accessed | tf_op | source)
XLA Modules:
  0.0 73.1 jit_solution(5566439479433925265)
XLA Ops:
  0.0 0.0 copy-start
  0.1 0.0 copy-start.6
  0.1 0.7 copy-done.6
  0.8 0.0 copy-start.5
  0.8 0.7 copy-done.5
  1.4 0.3 reduce-window.9
  1.7 0.1 slice.23
  1.9 0.1 slice_reduce_fusion
  2.0 0.0 copy-start.1
  2.0 0.0 copy-start.2
  2.0 1.1 %copy.49 = bf16[256,512]{0,1:T(8,128)(2,1)S(1)} copy(bf16[256,512]{1,0:T(8,128)(2,1)} %param.9) | data formatting | bytes 524288 | tf_op jit(solution)/shard_map/reshape | solution.py:56
  3.1 0.0 copy-start.4
  3.2 0.7 copy-done.4
  3.8 0.1 select_reduce_fusion
  4.0 0.7 fusion.31
  4.7 0.2 convert_reduce_fusion
  4.8 0.2 convert_reduce_fusion.2
  5.1 0.1 exponential_select_fusion.3
  5.2 0.7 broadcast_compare_fusion.1
  5.9 0.1 exponential_select_fusion.2
  5.9 0.0 copy-done.1
  6.0 0.0 copy-done.2
  6.0 0.4 convolution_add_fusion
  6.4 4.4 %collective-permute-start.3 = (f32[4,128,128]{2,1,0:T(8,128)S(1)}, f32[4,128,128]{2,1,0:T(8,128)S(1)}, u32[]{:S(2)}, u32[]{:S(2)}) collective-permute-start(f32[4,128,128]{2,1,0:T(8,128)S(1)} %convolution_add_fusion), channel_id=1, source_target_pairs={{0,32},{8,40},{16,48},{24,56},{32,64},{40,72},{48,80},{56,88},{64,... | collective-permute-start | bytes 786440 | tf_op jit(solution)/shard_map/ppermute | solution.py:11
  10.8 4.6 %collective-permute-start.2 = (f32[4,128,128]{2,1,0:T(8,128)S(1)}, f32[4,128,128]{2,1,0:T(8,128)S(1)}, u32[]{:S(2)}, u32[]{:S(2)}) collective-permute-start(f32[4,128,128]{2,1,0:T(8,128)S(1)} %convolution_add_fusion), channel_id=1, source_target_pairs={{0,24},{8,32},{16,40},{24,48},{32,56},{40,64},{48,72},{56,80},{64,... | collective-permute-start | bytes 786440 | tf_op jit(solution)/shard_map/ppermute | solution.py:11
  15.4 3.6 %collective-permute-start.1 = (f32[4,128,128]{2,1,0:T(8,128)S(1)}, f32[4,128,128]{2,1,0:T(8,128)S(1)}, u32[]{:S(2)}, u32[]{:S(2)}) collective-permute-start(f32[4,128,128]{2,1,0:T(8,128)S(1)} %convolution_add_fusion), channel_id=1, source_target_pairs={{0,16},{8,24},{16,32},{24,40},{32,48},{40,56},{48,64},{56,72},{64,... | collective-permute-start | bytes 786440 | tf_op jit(solution)/shard_map/ppermute | solution.py:11
  19.0 2.6 %collective-permute-start = (f32[4,128,128]{2,1,0:T(8,128)S(1)}, f32[4,128,128]{2,1,0:T(8,128)S(1)}, u32[]{:S(2)}, u32[]{:S(2)}) collective-permute-start(f32[4,128,128]{2,1,0:T(8,128)S(1)} %convolution_add_fusion), channel_id=1, source_target_pairs={{0,8},{8,16},{16,24},{24,32},{32,40},{40,48},{48,56},{56,64},{64,7... | collective-permute-start | bytes 786440 | tf_op jit(solution)/shard_map/ppermute | solution.py:11
  21.6 0.1 fusion.7
  21.7 0.1 fusion.20
  21.9 0.0 copy-done
  21.9 0.4 fusion.4
  22.4 0.3 fusion
  22.7 0.0 collective-permute-done.3
  22.7 11.2 %collective-permute-done.2 = f32[4,128,128]{2,1,0:T(8,128)S(1)} collective-permute-done((f32[4,128,128]{2,1,0:T(8,128)S(1)}, f32[4,128,128]{2,1,0:T(8,128)S(1)}, u32[]{:S(2)}, u32[]{:S(2)}) %collective-permute-start.2) | collective-permute-done | bytes 262176 | tf_op jit(solution)/shard_map/ppermute | solution.py:11
  33.9 6.5 %collective-permute-done.1 = f32[4,128,128]{2,1,0:T(8,128)S(1)} collective-permute-done((f32[4,128,128]{2,1,0:T(8,128)S(1)}, f32[4,128,128]{2,1,0:T(8,128)S(1)}, u32[]{:S(2)}, u32[]{:S(2)}) %collective-permute-start.1) | collective-permute-done | bytes 262176 | tf_op jit(solution)/shard_map/ppermute | solution.py:11
  40.5 1.7 %collective-permute-done = f32[4,128,128]{2,1,0:T(8,128)S(1)} collective-permute-done((f32[4,128,128]{2,1,0:T(8,128)S(1)}, f32[4,128,128]{2,1,0:T(8,128)S(1)}, u32[]{:S(2)}, u32[]{:S(2)}) %collective-permute-start) | collective-permute-done | bytes 262176 | tf_op jit(solution)/shard_map/ppermute | solution.py:11
  42.1 0.1 multiply_add_fusion
  42.3 1.9 %collective-permute-start.4 = (f32[4,128,128]{2,1,0:T(8,128)S(1)}, f32[4,128,128]{2,1,0:T(8,128)S(1)}, u32[]{:S(2)}, u32[]{:S(2)}) collective-permute-start(f32[4,128,128]{2,1,0:T(8,128)S(1)} %multiply_add_fusion), channel_id=1, source_target_pairs={{0,32},{8,40},{16,48},{24,56},{32,64},{40,72},{48,80},{56,88},{64,... | collective-permute-start | bytes 786440 | tf_op jit(solution)/shard_map/ppermute | solution.py:11
  44.2 0.7 convolution_bitcast_fusion.2
  44.9 14.3 %collective-permute-done.4 = f32[4,128,128]{2,1,0:T(8,128)S(1)} collective-permute-done((f32[4,128,128]{2,1,0:T(8,128)S(1)}, f32[4,128,128]{2,1,0:T(8,128)S(1)}, u32[]{:S(2)}, u32[]{:S(2)}) %collective-permute-start.4) | collective-permute-done | bytes 262176 | tf_op jit(solution)/shard_map/ppermute | solution.py:11
  59.2 0.6 multiply_reduce_fusion
  59.8 0.6 broadcast_in_dim.118
  60.4 6.5 %all-to-all-start = ((f32[8,1,256]{2,1,0:T(1,128)}), f32[8,1,256]{2,1,0:T(1,128)S(1)}, u32[]{:S(2)}, u32[]{:S(2)}) async-start(f32[8,1,256]{2,1,0:T(1,128)} %broadcast_in_dim.118), calls=%async_computation | async-start | bytes 16384 | tf_op jit(solution)/shard_map/all_to_all | solution.py:111
  67.0 0.2 copy.45
  67.2 4.4 %all-to-all-done = f32[8,1,256]{2,1,0:T(1,128)S(1)} async-done(((f32[8,1,256]{2,1,0:T(1,128)}), f32[8,1,256]{2,1,0:T(1,128)S(1)}, u32[]{:S(2)}, u32[]{:S(2)}) %all-to-all-start) | async-done | bytes 8224 | tf_op jit(solution)/shard_map/all_to_all | solution.py:111
  71.6 0.0 copy-start.3
  71.6 0.7 copy-done.3
  72.3 0.8 %multiply_convert_fusion = bf16[256,512]{1,0:T(8,128)(2,1)} fusion(f32[256,512]{1,0:T(8,128)S(1)} %copy.45, f32[512]{0:T(512)S(1)} %copy-done.3, f32[256]{0:T(256)S(1)} %add_rsqrt_fusion), kind=kLoop, calls=%fused_computation.10 | loop fusion | flops 393216 | bytes 789504 | tf_op jit(solution)/shard_map/convert_element_type | solution.py:113
  (11 shorter events, 0.1 us)
Async XLA Ops:
  0.0 21.9 %copy-start = (bf16[256,512]{1,0:T(8,128)(2,1)S(1)}, bf16[256,512]{1,0:T(8,128)(2,1)}, u32[]{:S(2)}) copy-start(bf16[256,512]{1,0:T(8,128)(2,1)} %param.8) | copy-start | bytes 786436
  0.1 0.7 copy-start.6
  0.8 0.7 copy-start.5
  2.0 4.0 %copy-start.1 = (bf16[256,512]{1,0:T(8,128)(2,1)S(1)}, bf16[256,512]{1,0:T(8,128)(2,1)}, u32[]{:S(2)}) copy-start(bf16[256,512]{1,0:T(8,128)(2,1)} %param.10) | copy-start | bytes 786436
  2.0 4.0 %copy-start.2 = (f32[4,128,128]{2,1,0:T(8,128)S(1)}, f32[4,128,128]{2,1,0:T(8,128)}, u32[]{:S(2)}) copy-start(f32[4,128,128]{2,1,0:T(8,128)} %param.11) | copy-start | bytes 786436
  3.1 0.7 copy-start.4
  6.4 16.3 %collective-permute-start.3 = (f32[4,128,128]{2,1,0:T(8,128)S(1)}, f32[4,128,128]{2,1,0:T(8,128)S(1)}, u32[]{:S(2)}, u32[]{:S(2)}) collective-permute-start(f32[4,128,128]{2,1,0:T(8,128)S(1)} %convolution_add_fusion), channel_id=1, source_target_pairs={{0,32},{8,40},{16,48},{24,56},{32,64},{40,72},{48,80},{56,88},{64,... | collective-permute-start | bytes 786440 | tf_op jit(solution)/shard_map/ppermute | solution.py:11
  10.8 23.2 %collective-permute-start.2 = (f32[4,128,128]{2,1,0:T(8,128)S(1)}, f32[4,128,128]{2,1,0:T(8,128)S(1)}, u32[]{:S(2)}, u32[]{:S(2)}) collective-permute-start(f32[4,128,128]{2,1,0:T(8,128)S(1)} %convolution_add_fusion), channel_id=1, source_target_pairs={{0,24},{8,32},{16,40},{24,48},{32,56},{40,64},{48,72},{56,80},{64,... | collective-permute-start | bytes 786440 | tf_op jit(solution)/shard_map/ppermute | solution.py:11
  15.4 25.0 %collective-permute-start.1 = (f32[4,128,128]{2,1,0:T(8,128)S(1)}, f32[4,128,128]{2,1,0:T(8,128)S(1)}, u32[]{:S(2)}, u32[]{:S(2)}) collective-permute-start(f32[4,128,128]{2,1,0:T(8,128)S(1)} %convolution_add_fusion), channel_id=1, source_target_pairs={{0,16},{8,24},{16,32},{24,40},{32,48},{40,56},{48,64},{56,72},{64,... | collective-permute-start | bytes 786440 | tf_op jit(solution)/shard_map/ppermute | solution.py:11
  19.0 23.1 %collective-permute-start = (f32[4,128,128]{2,1,0:T(8,128)S(1)}, f32[4,128,128]{2,1,0:T(8,128)S(1)}, u32[]{:S(2)}, u32[]{:S(2)}) collective-permute-start(f32[4,128,128]{2,1,0:T(8,128)S(1)} %convolution_add_fusion), channel_id=1, source_target_pairs={{0,8},{8,16},{16,24},{24,32},{32,40},{40,48},{48,56},{56,64},{64,7... | collective-permute-start | bytes 786440 | tf_op jit(solution)/shard_map/ppermute | solution.py:11
  42.3 17.0 %collective-permute-start.4 = (f32[4,128,128]{2,1,0:T(8,128)S(1)}, f32[4,128,128]{2,1,0:T(8,128)S(1)}, u32[]{:S(2)}, u32[]{:S(2)}) collective-permute-start(f32[4,128,128]{2,1,0:T(8,128)S(1)} %multiply_add_fusion), channel_id=1, source_target_pairs={{0,32},{8,40},{16,48},{24,56},{32,64},{40,72},{48,80},{56,88},{64,... | collective-permute-start | bytes 786440 | tf_op jit(solution)/shard_map/ppermute | solution.py:11
  60.4 11.2 %all-to-all-start = ((f32[8,1,256]{2,1,0:T(1,128)}), f32[8,1,256]{2,1,0:T(1,128)S(1)}, u32[]{:S(2)}, u32[]{:S(2)}) async-start(f32[8,1,256]{2,1,0:T(1,128)} %broadcast_in_dim.118), calls=%async_computation | async-start | bytes 16384 | tf_op jit(solution)/shard_map/all_to_all | solution.py:111
  71.6 0.7 copy-start.3

commit v8 on v7

--- a/solution.py
+++ b/solution.py
@@ -90,6 +90,9 @@
     scores = jnp.einsum("thd,shd->hts", q, k, preferred_element_type=jnp.float32)
     weights = jnp.where(same_doc[None], scores * decay, jnp.float32(0.0))
     attn = jnp.einsum("hts,shd->thd", weights, v_f, precision=highest)
+    attn, gain_rows = lax.optimization_barrier(
+        (attn, jnp.broadcast_to(norm_gain[None, :], (row_count, feature_count)))
+    )
 
     lead_in = jnp.where(
         (segment == in_seg)[:, None],
@@ -110,7 +113,7 @@
     part = jnp.broadcast_to(jnp.sum(flat * flat, axis=1)[None], (groups, row_count))
     square_total = jnp.sum(lax.all_to_all(part, ("chip", "core"), 0, 0), axis=0)
     mean_sq = square_total / jnp.float32(feature_count * lax.axis_size("chip") * lax.axis_size("core"))
-    return (flat * lax.rsqrt(mean_sq + 1e-05)[:, None] * norm_gain[None, :]).astype(jnp.bfloat16)
+    return (flat * lax.rsqrt(mean_sq + 1e-05)[:, None] * gain_rows).astype(jnp.bfloat16)
 
 
 def solution(mesh):

time: 73.5 us -> 73 us (level)
  other arithmetic: 3.7 us -> 2.94 us
    convert_element_type x0 -> x1, local copies, waits for them, and re-layouts: none -> 0.84 us  [shards(): (flat * lax.rsqrt(mean_sq + 1e-05)[:, None] * gain_rows).astype(jnp.bfloa...]
    convert_element_type x1, other arithmetic: 0.82 us -> 0.07 us  [shards(): (flat * lax.rsqrt(mean_sq + 1e-05)[:, None] * gain_rows).astype(jnp.bfloa...]
where the time goes in v8:
time: 73 us; the launch traced here: 72.6 us
  waiting for transfers between devices  38.2 us (52%)
  starting transfers between devices  23.7 us (32%)
  local copies, waits for them, and re-layouts  5.18 us (7%)
  other arithmetic  2.94 us (4%)
  matrix products  2.36 us (3%)
    ppermute x5, waiting for transfers between devices, shifted(): return lax.ppermute(value, axis, pairs)  33.8 us
    ppermute x5, starting transfers between devices, shifted(): return lax.ppermute(value, axis, pairs)  17.2 us
    all_to_all x1, starting transfers between devices, shards(): square_total = jnp.sum(lax.all_to_all(part, ('chip', 'core'), 0, 0), axis=0)  6.55 us
    all_to_all x1, waiting for transfers between devices, shards(): square_total = jnp.sum(lax.all_to_all(part, ('chip', 'core'), 0, 0), axis=0)  4.41 us
    unnamed x14, local copies, waits for them, and re-layouts  2.06 us
  transfers between devices with their start and end apart: 6, of which 5 were waited for; matrix products, arithmetic and copies ran while one was open for 3% of the time, Pallas kernels for 0%

profile of v8, /device:TPU:1, one launch (start us, length us, event | category | flops | bytes accessed | tf_op | source)
XLA Modules:
  0.0 72.6 jit_solution(1321898348472307380)
XLA Ops:
  0.0 0.0 copy-start
  0.0 0.0 copy-start.6
  0.1 0.7 copy-done.6
  0.7 0.7 copy-done.5
  1.4 0.3 reduce-window.9
  1.7 0.1 slice.23
  1.8 0.1 slice_reduce_fusion
  2.0 0.7 fusion.33
  2.7 0.2 convert_reduce_fusion.2
  2.9 0.1 exponential_select_fusion.3
  3.0 0.7 copy-done.4
  3.7 0.1 select_reduce_fusion
  3.8 0.2 convert_reduce_fusion
  4.0 0.0 copy-start.1
  4.0 0.0 copy-start.2
  4.0 1.1 %copy.61 = bf16[256,512]{0,1:T(8,128)(2,1)S(1)} copy(bf16[256,512]{1,0:T(8,128)(2,1)} %param.9) | data formatting | bytes 524288 | tf_op jit(solution)/shard_map/reshape | solution.py:56
  5.1 0.7 broadcast_compare_fusion.1
  5.8 0.1 exponential_select_fusion.2
  5.9 0.0 copy-done.1
  5.9 0.0 copy-done.2
  5.9 0.4 convolution_add_fusion
  6.3 4.4 %collective-permute-start.3 = (f32[4,128,128]{2,1,0:T(8,128)S(1)}, f32[4,128,128]{2,1,0:T(8,128)S(1)}, u32[]{:S(2)}, u32[]{:S(2)}) collective-permute-start(f32[4,128,128]{2,1,0:T(8,128)S(1)} %convolution_add_fusion), channel_id=1, source_target_pairs={{0,32},{8,40},{16,48},{24,56},{32,64},{40,72},{48,80},{56,88},{64,... | collective-permute-start | bytes 786440 | tf_op jit(solution)/shard_map/ppermute | solution.py:11
  10.7 4.6 %collective-permute-start.2 = (f32[4,128,128]{2,1,0:T(8,128)S(1)}, f32[4,128,128]{2,1,0:T(8,128)S(1)}, u32[]{:S(2)}, u32[]{:S(2)}) collective-permute-start(f32[4,128,128]{2,1,0:T(8,128)S(1)} %convolution_add_fusion), channel_id=1, source_target_pairs={{0,24},{8,32},{16,40},{24,48},{32,56},{40,64},{48,72},{56,80},{64,... | collective-permute-start | bytes 786440 | tf_op jit(solution)/shard_map/ppermute | solution.py:11
  15.4 3.6 %collective-permute-start.1 = (f32[4,128,128]{2,1,0:T(8,128)S(1)}, f32[4,128,128]{2,1,0:T(8,128)S(1)}, u32[]{:S(2)}, u32[]{:S(2)}) collective-permute-start(f32[4,128,128]{2,1,0:T(8,128)S(1)} %convolution_add_fusion), channel_id=1, source_target_pairs={{0,16},{8,24},{16,32},{24,40},{32,48},{40,56},{48,64},{56,72},{64,... | collective-permute-start | bytes 786440 | tf_op jit(solution)/shard_map/ppermute | solution.py:11
  19.0 2.6 %collective-permute-start = (f32[4,128,128]{2,1,0:T(8,128)S(1)}, f32[4,128,128]{2,1,0:T(8,128)S(1)}, u32[]{:S(2)}, u32[]{:S(2)}) collective-permute-start(f32[4,128,128]{2,1,0:T(8,128)S(1)} %convolution_add_fusion), channel_id=1, source_target_pairs={{0,8},{8,16},{16,24},{24,32},{32,40},{40,48},{48,56},{56,64},{64,7... | collective-permute-start | bytes 786440 | tf_op jit(solution)/shard_map/ppermute | solution.py:11
  21.6 0.1 fusion.22
  21.8 0.1 fusion.9
  21.9 0.0 copy-done
  21.9 0.3 fusion
  22.2 0.0 collective-permute-done.3
  22.3 11.7 %collective-permute-done.2 = f32[4,128,128]{2,1,0:T(8,128)S(1)} collective-permute-done((f32[4,128,128]{2,1,0:T(8,128)S(1)}, f32[4,128,128]{2,1,0:T(8,128)S(1)}, u32[]{:S(2)}, u32[]{:S(2)}) %collective-permute-start.2) | collective-permute-done | bytes 262176 | tf_op jit(solution)/shard_map/ppermute | solution.py:11
  33.9 6.5 %collective-permute-done.1 = f32[4,128,128]{2,1,0:T(8,128)S(1)} collective-permute-done((f32[4,128,128]{2,1,0:T(8,128)S(1)}, f32[4,128,128]{2,1,0:T(8,128)S(1)}, u32[]{:S(2)}, u32[]{:S(2)}) %collective-permute-start.1) | collective-permute-done | bytes 262176 | tf_op jit(solution)/shard_map/ppermute | solution.py:11
  40.4 1.6 %collective-permute-done = f32[4,128,128]{2,1,0:T(8,128)S(1)} collective-permute-done((f32[4,128,128]{2,1,0:T(8,128)S(1)}, f32[4,128,128]{2,1,0:T(8,128)S(1)}, u32[]{:S(2)}, u32[]{:S(2)}) %collective-permute-start) | collective-permute-done | bytes 262176 | tf_op jit(solution)/shard_map/ppermute | solution.py:11
  42.1 0.1 multiply_add_fusion
  42.2 0.0 copy-start.3
  42.2 1.9 %collective-permute-start.4 = (f32[4,128,128]{2,1,0:T(8,128)S(1)}, f32[4,128,128]{2,1,0:T(8,128)S(1)}, u32[]{:S(2)}, u32[]{:S(2)}) collective-permute-start(f32[4,128,128]{2,1,0:T(8,128)S(1)} %multiply_add_fusion), channel_id=1, source_target_pairs={{0,32},{8,40},{16,48},{24,56},{32,64},{40,72},{48,80},{56,88},{64,... | collective-permute-start | bytes 786440 | tf_op jit(solution)/shard_map/ppermute | solution.py:11
  44.1 0.6 convolution_bitcast_fusion.2
  44.8 0.0 copy-done.3
  44.8 0.1 broadcast_in_dim.76
  44.9 0.4 fusion.4
  45.3 14.0 %collective-permute-done.4 = f32[4,128,128]{2,1,0:T(8,128)S(1)} collective-permute-done((f32[4,128,128]{2,1,0:T(8,128)S(1)}, f32[4,128,128]{2,1,0:T(8,128)S(1)}, u32[]{:S(2)}, u32[]{:S(2)}) %collective-permute-start.4) | collective-permute-done | bytes 262176 | tf_op jit(solution)/shard_map/ppermute | solution.py:11
  59.2 0.6 multiply_reduce_fusion
  59.9 0.6 broadcast_in_dim.124
  60.5 6.5 %all-to-all-start = ((f32[8,1,256]{2,1,0:T(1,128)}), f32[8,1,256]{2,1,0:T(1,128)S(1)}, u32[]{:S(2)}, u32[]{:S(2)}) async-start(f32[8,1,256]{2,1,0:T(1,128)} %broadcast_in_dim.124), calls=%async_computation | async-start | bytes 16384 | tf_op jit(solution)/shard_map/all_to_all | solution.py:114
  67.0 0.2 copy.53
  67.2 4.4 %all-to-all-done = f32[8,1,256]{2,1,0:T(1,128)S(1)} async-done(((f32[8,1,256]{2,1,0:T(1,128)}), f32[8,1,256]{2,1,0:T(1,128)S(1)}, u32[]{:S(2)}, u32[]{:S(2)}) %all-to-all-start) | async-done | bytes 8224 | tf_op jit(solution)/shard_map/all_to_all | solution.py:114
  71.7 0.1 fusion.6
  71.8 0.8 %copy.55 = bf16[256,512]{1,0:T(8,128)(2,1)} copy(bf16[256,512]{0,1:T(8,128)(2,1)S(1)} %fusion.6) | data formatting | bytes 524288 | tf_op jit(solution)/shard_map/convert_element_type | solution.py:116
  (13 shorter events, 0.1 us)
Async XLA Ops:
  0.0 21.9 %copy-start = (bf16[256,512]{1,0:T(8,128)(2,1)S(1)}, bf16[256,512]{1,0:T(8,128)(2,1)}, u32[]{:S(2)}) copy-start(bf16[256,512]{1,0:T(8,128)(2,1)} %param.8) | copy-start | bytes 786436
  0.0 0.7 copy-start.6
  0.7 0.7 copy-start.5
  3.0 0.7 copy-start.4
  4.0 1.9 %copy-start.1 = (bf16[256,512]{1,0:T(8,128)(2,1)S(1)}, bf16[256,512]{1,0:T(8,128)(2,1)}, u32[]{:S(2)}) copy-start(bf16[256,512]{1,0:T(8,128)(2,1)} %param.10) | copy-start | bytes 786436
  4.0 1.9 %copy-start.2 = (f32[4,128,128]{2,1,0:T(8,128)S(1)}, f32[4,128,128]{2,1,0:T(8,128)}, u32[]{:S(2)}) copy-start(f32[4,128,128]{2,1,0:T(8,128)} %param.11) | copy-start | bytes 786436
  6.3 15.9 %collective-permute-start.3 = (f32[4,128,128]{2,1,0:T(8,128)S(1)}, f32[4,128,128]{2,1,0:T(8,128)S(1)}, u32[]{:S(2)}, u32[]{:S(2)}) collective-permute-start(f32[4,128,128]{2,1,0:T(8,128)S(1)} %convolution_add_fusion), channel_id=1, source_target_pairs={{0,32},{8,40},{16,48},{24,56},{32,64},{40,72},{48,80},{56,88},{64,... | collective-permute-start | bytes 786440 | tf_op jit(solution)/shard_map/ppermute | solution.py:11
  10.7 23.2 %collective-permute-start.2 = (f32[4,128,128]{2,1,0:T(8,128)S(1)}, f32[4,128,128]{2,1,0:T(8,128)S(1)}, u32[]{:S(2)}, u32[]{:S(2)}) collective-permute-start(f32[4,128,128]{2,1,0:T(8,128)S(1)} %convolution_add_fusion), channel_id=1, source_target_pairs={{0,24},{8,32},{16,40},{24,48},{32,56},{40,64},{48,72},{56,80},{64,... | collective-permute-start | bytes 786440 | tf_op jit(solution)/shard_map/ppermute | solution.py:11
  15.4 25.0 %collective-permute-start.1 = (f32[4,128,128]{2,1,0:T(8,128)S(1)}, f32[4,128,128]{2,1,0:T(8,128)S(1)}, u32[]{:S(2)}, u32[]{:S(2)}) collective-permute-start(f32[4,128,128]{2,1,0:T(8,128)S(1)} %convolution_add_fusion), channel_id=1, source_target_pairs={{0,16},{8,24},{16,32},{24,40},{32,48},{40,56},{48,64},{56,72},{64,... | collective-permute-start | bytes 786440 | tf_op jit(solution)/shard_map/ppermute | solution.py:11
  19.0 23.0 %collective-permute-start = (f32[4,128,128]{2,1,0:T(8,128)S(1)}, f32[4,128,128]{2,1,0:T(8,128)S(1)}, u32[]{:S(2)}, u32[]{:S(2)}) collective-permute-start(f32[4,128,128]{2,1,0:T(8,128)S(1)} %convolution_add_fusion), channel_id=1, source_target_pairs={{0,8},{8,16},{16,24},{24,32},{32,40},{40,48},{48,56},{56,64},{64,7... | collective-permute-start | bytes 786440 | tf_op jit(solution)/shard_map/ppermute | solution.py:11
  42.2 2.6 %copy-start.3 = (f32[512]{0:T(512)S(1)}, f32[512]{0:T(512)}, u32[]{:S(2)}) copy-start(f32[512]{0:T(512)} %param.13) | copy-start | bytes 6148
  42.2 17.0 %collective-permute-start.4 = (f32[4,128,128]{2,1,0:T(8,128)S(1)}, f32[4,128,128]{2,1,0:T(8,128)S(1)}, u32[]{:S(2)}, u32[]{:S(2)}) collective-permute-start(f32[4,128,128]{2,1,0:T(8,128)S(1)} %multiply_add_fusion), channel_id=1, source_target_pairs={{0,32},{8,40},{16,48},{24,56},{32,64},{40,72},{48,80},{56,88},{64,... | collective-permute-start | bytes 786440 | tf_op jit(solution)/shard_map/ppermute | solution.py:11
  60.5 11.2 %all-to-all-start = ((f32[8,1,256]{2,1,0:T(1,128)}), f32[8,1,256]{2,1,0:T(1,128)S(1)}, u32[]{:S(2)}, u32[]{:S(2)}) async-start(f32[8,1,256]{2,1,0:T(1,128)} %broadcast_in_dim.124), calls=%async_computation | async-start | bytes 16384 | tf_op jit(solution)/shard_map/all_to_all | solution.py:114

commit v9 on v6

--- a/solution.py
+++ b/solution.py
@@ -69,17 +69,21 @@
     initial = carry_state * (device == 0).astype(jnp.float32)
     element = through[0][:, None, None] * initial + running
 
+    e1 = shifted(element, "ctx", 1)
+    e2 = shifted(element, "ctx", 2)
+    e3 = shifted(element, "ctx", 3)
+    e4 = shifted(element, "ctx", 4)
+    t0, t1, t2, t3, t4, t5 = (through[i][:, None, None] for i in range(6))
+    reach2 = t0 * t1
+    upto3 = element + t0 * e1 + reach2 * e2
+    five = upto3 + reach2 * t2 * e3 + reach2 * t2 * t3 * e4
+    three = e1 + t1 * e2 + t1 * t2 * e3
     last = ctx_count - 1
-    e1 = shifted(element, "ctx", 1, wrap_sources=(last,))
-    e2 = shifted(element, "ctx", 2, wrap_sources=(last - 1,))
-    t0, t1, t2, t3, t4, t5 = (through[i][:, None, None] for i in range(6))
-    reach1 = t0 * (device != 0).astype(jnp.float32)
-    three = element + reach1 * e1 + reach1 * t1 * e2
-    two = e1 + t1 * e2
-    mid = shifted(three, "ctx", 3, wrap_sources=(last - 2,))
-    far = shifted(three, "ctx", 6, wrap_sources=(last - 5,))
-    span2 = t1 * t2
-    incoming = two + span2 * mid + span2 * t3 * t4 * t5 * far
+    far = lax.ppermute(five, "ctx", [(s, s + 4) for s in range(ctx_count - 4)] + [(last, 0)])
+    tail = lax.ppermute(upto3, "ctx", [(last - 5, 0)])
+    first = (device == 0).astype(jnp.float32)
+    far_weight = first + (1.0 - first) * (t1 * t2 * t3)
+    incoming = three + far_weight * far + first * (t1 * t2 * t3 * t4 * t5) * tail
 
     distance = window[:, None] - window[None, :]
     same_doc = (segment[:, None] == segment[None, :]) & (distance >= 0)

time: 73.9 us -> 72.7 us (0.984)
  waiting for transfers between devices: 41.3 us -> 25.1 us
  starting transfers between devices: 21.1 us -> 35.9 us
    ppermute x4, waiting for transfers between devices: 36.8 us -> 2.39 us  [shifted(): return lax.ppermute(value, axis, pairs)]
    ppermute x0 -> x2, waiting for transfers between devices: none -> 18.3 us  [the longest x1 18.3 us: shards(): tail = lax.ppermute(upto3, 'ctx', [(last - 5, 0)])]
    ppermute x0 -> x2, starting transfers between devices: none -> 14.9 us  [the longest x1 13.6 us: shards(): lax.ppermute(five, 'ctx', [(s, s + 4) for s in range(ctx_count - 4)] + [(...]
    all_to_all x1, starting transfers between devices: 9.28 us -> 5.73 us  [shards(): square_total = jnp.sum(lax.all_to_all(part, ('chip', 'core'), 0, 0), axis=0)]
    ppermute x4, starting transfers between devices: 11.8 us -> 15.3 us  [shifted(): return lax.ppermute(value, axis, pairs)]
  transfers between devices with their start and end apart: 5 -> 7, of which waited for: 4 -> 3; matrix products, arithmetic and copies ran while one was open for 3% -> 3% of each run, Pallas kernels for 0% -> 0%
where the time goes in v9:
time: 72.7 us; the launch traced here: 72.3 us
  starting transfers between devices  35.9 us (49%)
  waiting for transfers between devices  25.1 us (35%)
  local copies, waits for them, and re-layouts  4.86 us (7%)
  other arithmetic  3.71 us (5%)
  matrix products  2.44 us (3%)
    ppermute x1, waiting for transfers between devices, shards(): tail = lax.ppermute(upto3, 'ctx', [(last - 5, 0)])  18.3 us
    ppermute x4, starting transfers between devices, shifted(): return lax.ppermute(value, axis, pairs)  15.3 us
    ppermute x1, starting transfers between devices, shards(): lax.ppermute(five, 'ctx', [(s, s + 4) for s in range(ctx_count - 4)] + [(...  13.6 us
    all_to_all x1, starting transfers between devices, shards(): square_total = jnp.sum(lax.all_to_all(part, ('chip', 'core'), 0, 0), axis=0)  5.73 us
    all_to_all x1, waiting for transfers between devices, shards(): square_total = jnp.sum(lax.all_to_all(part, ('chip', 'core'), 0, 0), axis=0)  4.41 us
    unnamed x14, local copies, waits for them, and re-layouts  2.72 us
    ppermute x4, waiting for transfers between devices, shifted(): return lax.ppermute(value, axis, pairs)  2.39 us
  transfers between devices with their start and end apart: 7, of which 3 were waited for; matrix products, arithmetic and copies ran while one was open for 3% of the time, Pallas kernels for 0%

profile of v9, /device:TPU:1, one launch (start us, length us, event | category | flops | bytes accessed | tf_op | source)
XLA Modules:
  0.0 72.3 jit_solution(17091701271974364766)
XLA Ops:
  0.0 0.0 copy-start
  0.1 0.0 copy-start.6
  0.1 0.7 copy-done.6
  0.8 0.7 copy-done.5
  1.4 0.3 reduce-window.9
  1.7 0.1 slice.29
  1.9 0.1 slice_reduce_fusion
  2.0 0.0 copy-start.1
  2.0 0.0 copy-start.2
  2.0 1.1 %copy.49 = bf16[256,512]{0,1:T(8,128)(2,1)S(1)} copy(bf16[256,512]{1,0:T(8,128)(2,1)} %param.9) | data formatting | bytes 524288 | tf_op jit(solution)/shard_map/reshape | solution.py:56
  3.1 0.0 copy-start.4
  3.2 0.7 copy-done.4
  3.8 0.1 select_reduce_fusion
  4.0 0.7 fusion.34
  4.7 0.2 convert_reduce_fusion
  4.8 0.2 convert_reduce_fusion.2
  5.1 0.1 exponential_select_fusion.3
  5.2 0.7 broadcast_compare_fusion.1
  5.9 0.1 exponential_select_fusion.2
  5.9 0.0 copy-done.1
  6.0 0.0 copy-done.2
  6.0 0.4 convolution_add_fusion
  6.4 4.4 %collective-permute-start.3 = (f32[4,128,128]{2,1,0:T(8,128)S(1)}, f32[4,128,128]{2,1,0:T(8,128)S(1)}, u32[]{:S(2)}, u32[]{:S(2)}) collective-permute-start(f32[4,128,128]{2,1,0:T(8,128)S(1)} %convolution_add_fusion), channel_id=1, source_target_pairs={{0,32},{8,40},{16,48},{24,56},{32,64},{40,72},{48,80},{56,88},{64,... | collective-permute-start | bytes 786440 | tf_op jit(solution)/shard_map/ppermute | solution.py:11
  10.8 4.7 %collective-permute-start.2 = (f32[4,128,128]{2,1,0:T(8,128)S(1)}, f32[4,128,128]{2,1,0:T(8,128)S(1)}, u32[]{:S(2)}, u32[]{:S(2)}) collective-permute-start(f32[4,128,128]{2,1,0:T(8,128)S(1)} %convolution_add_fusion), channel_id=1, source_target_pairs={{0,24},{8,32},{16,40},{24,48},{32,56},{40,64},{48,72},{56,80},{64,... | collective-permute-start | bytes 786440 | tf_op jit(solution)/shard_map/ppermute | solution.py:11
  15.4 3.6 %collective-permute-start.1 = (f32[4,128,128]{2,1,0:T(8,128)S(1)}, f32[4,128,128]{2,1,0:T(8,128)S(1)}, u32[]{:S(2)}, u32[]{:S(2)}) collective-permute-start(f32[4,128,128]{2,1,0:T(8,128)S(1)} %convolution_add_fusion), channel_id=1, source_target_pairs={{0,16},{8,24},{16,32},{24,40},{32,48},{40,56},{48,64},{56,72},{64,... | collective-permute-start | bytes 786440 | tf_op jit(solution)/shard_map/ppermute | solution.py:11
  19.0 2.6 %collective-permute-start = (f32[4,128,128]{2,1,0:T(8,128)S(1)}, f32[4,128,128]{2,1,0:T(8,128)S(1)}, u32[]{:S(2)}, u32[]{:S(2)}) collective-permute-start(f32[4,128,128]{2,1,0:T(8,128)S(1)} %convolution_add_fusion), channel_id=1, source_target_pairs={{0,8},{8,16},{16,24},{24,32},{32,40},{40,48},{48,56},{56,64},{64,7... | collective-permute-start | bytes 786440 | tf_op jit(solution)/shard_map/ppermute | solution.py:11
  21.7 0.1 fusion.7
  21.8 0.1 fusion.22
  21.9 0.0 copy-done
  21.9 0.4 fusion.4
  22.4 0.3 fusion
  22.7 0.0 collective-permute-done.3
  22.7 0.0 collective-permute-done.2
  22.7 0.0 collective-permute-done.1
  22.8 2.4 %collective-permute-done = f32[4,128,128]{2,1,0:T(8,128)S(1)} collective-permute-done((f32[4,128,128]{2,1,0:T(8,128)S(1)}, f32[4,128,128]{2,1,0:T(8,128)S(1)}, u32[]{:S(2)}, u32[]{:S(2)}) %collective-permute-start) | collective-permute-done | bytes 262176 | tf_op jit(solution)/shard_map/ppermute | solution.py:11
  25.1 0.1 multiply_add_fusion
  25.3 1.3 %collective-permute-start.5 = (f32[4,128,128]{2,1,0:T(8,128)S(1)}, f32[4,128,128]{2,1,0:T(8,128)S(1)}, u32[]{:S(2)}, u32[]{:S(2)}) collective-permute-start(f32[4,128,128]{2,1,0:T(8,128)S(1)} %get-tuple-element.10), channel_id=1, source_target_pairs={{976,0},{977,1},{978,2},{979,3},{980,4},{981,5},{982,6},{983,7}} | collective-permute-start | bytes 786440 | tf_op jit(solution)/shard_map/ppermute | solution.py:83
  26.6 13.6 %collective-permute-start.4 = (f32[4,128,128]{2,1,0:T(8,128)S(1)}, f32[4,128,128]{2,1,0:T(8,128)S(1)}, u32[]{:S(2)}, u32[]{:S(2)}) collective-permute-start(f32[4,128,128]{2,1,0:T(8,128)S(1)} %get-tuple-element.9), channel_id=1, source_target_pairs={{0,32},{8,40},{16,48},{24,56},{32,64},{40,72},{48,80},{56,88},{64,... | collective-permute-start | bytes 786440 | tf_op jit(solution)/shard_map/ppermute | solution.py:82
  40.2 0.7 %convolution_bitcast_fusion.2 = f32[256,4,128]{0,2,1:T(8,128)S(1)} fusion(f32[4,256,256]{2,1,0:T(8,128)S(1)} %fusion, bf16[256,512]{1,0:T(8,128)(2,1)S(1)} %copy-done.1), kind=kOutput, calls=%fused_computation.4 | convolution fusion | flops 402653184 | bytes 1835008 | tf_op jit(solution)/shard_map/hts,shd->thd/dot_general | solution.py:93
  40.9 18.3 %collective-permute-done.5 = f32[4,128,128]{2,1,0:T(8,128)S(1)} collective-permute-done((f32[4,128,128]{2,1,0:T(8,128)S(1)}, f32[4,128,128]{2,1,0:T(8,128)S(1)}, u32[]{:S(2)}, u32[]{:S(2)}) %collective-permute-start.5) | collective-permute-done | bytes 262176 | tf_op jit(solution)/shard_map/ppermute | solution.py:83
  59.2 0.0 collective-permute-done.4
  59.3 0.6 multiply_reduce_fusion
  59.8 0.6 broadcast_in_dim.118
  60.4 5.7 %all-to-all-start = ((f32[8,1,256]{2,1,0:T(1,128)}), f32[8,1,256]{2,1,0:T(1,128)S(1)}, u32[]{:S(2)}, u32[]{:S(2)}) async-start(f32[8,1,256]{2,1,0:T(1,128)} %broadcast_in_dim.118), calls=%async_computation | async-start | bytes 16384 | tf_op jit(solution)/shard_map/all_to_all | solution.py:112
  66.2 0.2 copy.45
  66.4 4.4 %all-to-all-done = f32[8,1,256]{2,1,0:T(1,128)S(1)} async-done(((f32[8,1,256]{2,1,0:T(1,128)}), f32[8,1,256]{2,1,0:T(1,128)S(1)}, u32[]{:S(2)}, u32[]{:S(2)}) %all-to-all-start) | async-done | bytes 8224 | tf_op jit(solution)/shard_map/all_to_all | solution.py:112
  70.8 0.7 copy-done.3
  71.5 0.8 %multiply_convert_fusion = bf16[256,512]{1,0:T(8,128)(2,1)} fusion(f32[256,512]{1,0:T(8,128)S(1)} %copy.45, f32[512]{0:T(512)S(1)} %copy-done.3, f32[256]{0:T(256)S(1)} %add_rsqrt_fusion), kind=kLoop, calls=%fused_computation.10 | loop fusion | flops 393216 | bytes 789504 | tf_op jit(solution)/shard_map/convert_element_type | solution.py:114
  (14 shorter events, 0.2 us)
Async XLA Ops:
  0.0 21.9 %copy-start = (bf16[256,512]{1,0:T(8,128)(2,1)S(1)}, bf16[256,512]{1,0:T(8,128)(2,1)}, u32[]{:S(2)}) copy-start(bf16[256,512]{1,0:T(8,128)(2,1)} %param.8) | copy-start | bytes 786436
  0.1 0.7 copy-start.6
  0.8 0.7 copy-start.5
  2.0 4.0 %copy-start.1 = (bf16[256,512]{1,0:T(8,128)(2,1)S(1)}, bf16[256,512]{1,0:T(8,128)(2,1)}, u32[]{:S(2)}) copy-start(bf16[256,512]{1,0:T(8,128)(2,1)} %param.10) | copy-start | bytes 786436
  2.0 4.0 %copy-start.2 = (f32[4,128,128]{2,1,0:T(8,128)S(1)}, f32[4,128,128]{2,1,0:T(8,128)}, u32[]{:S(2)}) copy-start(f32[4,128,128]{2,1,0:T(8,128)} %param.11) | copy-start | bytes 786436
  3.1 0.7 copy-start.4
  6.4 16.4 %collective-permute-start.3 = (f32[4,128,128]{2,1,0:T(8,128)S(1)}, f32[4,128,128]{2,1,0:T(8,128)S(1)}, u32[]{:S(2)}, u32[]{:S(2)}) collective-permute-start(f32[4,128,128]{2,1,0:T(8,128)S(1)} %convolution_add_fusion), channel_id=1, source_target_pairs={{0,32},{8,40},{16,48},{24,56},{32,64},{40,72},{48,80},{56,88},{64,... | collective-permute-start | bytes 786440 | tf_op jit(solution)/shard_map/ppermute | solution.py:11
  10.8 12.0 %collective-permute-start.2 = (f32[4,128,128]{2,1,0:T(8,128)S(1)}, f32[4,128,128]{2,1,0:T(8,128)S(1)}, u32[]{:S(2)}, u32[]{:S(2)}) collective-permute-start(f32[4,128,128]{2,1,0:T(8,128)S(1)} %convolution_add_fusion), channel_id=1, source_target_pairs={{0,24},{8,32},{16,40},{24,48},{32,56},{40,64},{48,72},{56,80},{64,... | collective-permute-start | bytes 786440 | tf_op jit(solution)/shard_map/ppermute | solution.py:11
  15.4 7.3 %collective-permute-start.1 = (f32[4,128,128]{2,1,0:T(8,128)S(1)}, f32[4,128,128]{2,1,0:T(8,128)S(1)}, u32[]{:S(2)}, u32[]{:S(2)}) collective-permute-start(f32[4,128,128]{2,1,0:T(8,128)S(1)} %convolution_add_fusion), channel_id=1, source_target_pairs={{0,16},{8,24},{16,32},{24,40},{32,48},{40,56},{48,64},{56,72},{64,... | collective-permute-start | bytes 786440 | tf_op jit(solution)/shard_map/ppermute | solution.py:11
  19.0 6.1 %collective-permute-start = (f32[4,128,128]{2,1,0:T(8,128)S(1)}, f32[4,128,128]{2,1,0:T(8,128)S(1)}, u32[]{:S(2)}, u32[]{:S(2)}) collective-permute-start(f32[4,128,128]{2,1,0:T(8,128)S(1)} %convolution_add_fusion), channel_id=1, source_target_pairs={{0,8},{8,16},{16,24},{24,32},{32,40},{40,48},{48,56},{56,64},{64,7... | collective-permute-start | bytes 786440 | tf_op jit(solution)/shard_map/ppermute | solution.py:11
  25.3 34.0 %collective-permute-start.5 = (f32[4,128,128]{2,1,0:T(8,128)S(1)}, f32[4,128,128]{2,1,0:T(8,128)S(1)}, u32[]{:S(2)}, u32[]{:S(2)}) collective-permute-start(f32[4,128,128]{2,1,0:T(8,128)S(1)} %get-tuple-element.10), channel_id=1, source_target_pairs={{976,0},{977,1},{978,2},{979,3},{980,4},{981,5},{982,6},{983,7}} | collective-permute-start | bytes 786440 | tf_op jit(solution)/shard_map/ppermute | solution.py:83
  26.6 32.7 %collective-permute-start.4 = (f32[4,128,128]{2,1,0:T(8,128)S(1)}, f32[4,128,128]{2,1,0:T(8,128)S(1)}, u32[]{:S(2)}, u32[]{:S(2)}) collective-permute-start(f32[4,128,128]{2,1,0:T(8,128)S(1)} %get-tuple-element.9), channel_id=1, source_target_pairs={{0,32},{8,40},{16,48},{24,56},{32,64},{40,72},{48,80},{56,88},{64,... | collective-permute-start | bytes 786440 | tf_op jit(solution)/shard_map/ppermute | solution.py:82
  60.4 10.3 %all-to-all-start = ((f32[8,1,256]{2,1,0:T(1,128)}), f32[8,1,256]{2,1,0:T(1,128)S(1)}, u32[]{:S(2)}, u32[]{:S(2)}) async-start(f32[8,1,256]{2,1,0:T(1,128)} %broadcast_in_dim.118), calls=%async_computation | async-start | bytes 16384 | tf_op jit(solution)/shard_map/all_to_all | solution.py:112
  70.8 0.7 copy-start.3

commit v10 on v9

--- a/solution.py
+++ b/solution.py
@@ -47,7 +47,7 @@
         )
         return end_seg, through
 
-    near = (device - jnp.arange(6, dtype=jnp.int32)) % ctx_count
+    near = (device - jnp.arange(4, dtype=jnp.int32)) % ctx_count
     end_segs, through = window_bounds(near)
     in_seg = doc_of(((device * row_count - spill_count - 1) % total)[None])[0]
     end_seg = end_segs[0]
@@ -73,17 +73,15 @@
     e2 = shifted(element, "ctx", 2)
     e3 = shifted(element, "ctx", 3)
     e4 = shifted(element, "ctx", 4)
-    t0, t1, t2, t3, t4, t5 = (through[i][:, None, None] for i in range(6))
+    t0, t1, t2, t3 = (through[i][:, None, None] for i in range(4))
     reach2 = t0 * t1
     upto3 = element + t0 * e1 + reach2 * e2
     five = upto3 + reach2 * t2 * e3 + reach2 * t2 * t3 * e4
     three = e1 + t1 * e2 + t1 * t2 * e3
     last = ctx_count - 1
-    far = lax.ppermute(five, "ctx", [(s, s + 4) for s in range(ctx_count - 4)] + [(last, 0)])
-    tail = lax.ppermute(upto3, "ctx", [(last - 5, 0)])
-    first = (device == 0).astype(jnp.float32)
-    far_weight = first + (1.0 - first) * (t1 * t2 * t3)
-    incoming = three + far_weight * far + first * (t1 * t2 * t3 * t4 * t5) * tail
+    far = lax.ppermute(five, "ctx", [(s, s + 4) for s in range(ctx_count - 4)] + [(last - 3, 0)])
+    tail = lax.ppermute(upto3, "ctx", [(last, 0)])
+    incoming = three + t1 * t2 * t3 * far + tail
 
     distance = window[:, None] - window[None, :]
     same_doc = (segment[:, None] == segment[None, :]) & (distance >= 0)

time: 72.7 us -> 74.2 us (1.021)
  starting transfers between devices: 35.9 us -> 36.7 us
    ppermute x1, waiting for transfers between devices: 0.01 us -> 8.27 us  [shards(): lax.ppermute(five, 'ctx', [(s, s + 4) for s in range(ctx_count - 4)] + [(...]
    ppermute x1, waiting for transfers between devices: 18.3 us -> 10.7 us  [shards(): tail = lax.ppermute(upto3, 'ctx', [(last, 0)])]
    all_to_all x1, starting transfers between devices: 5.73 us -> 6.54 us  [shards(): square_total = jnp.sum(lax.all_to_all(part, ('chip', 'core'), 0, 0), axis=0)]
  transfers between devices with their start and end apart: 7 -> 7, of which waited for: 3 -> 4; matrix products, arithmetic and copies ran while one was open for 3% -> 3% of each run, Pallas kernels for 0% -> 0%
where the time goes in v10:
time: 74.2 us; the launch traced here: 73.8 us
  starting transfers between devices  36.7 us (49%)
  waiting for transfers between devices  25.8 us (35%)
  local copies, waits for them, and re-layouts  4.86 us (7%)
  other arithmetic  3.7 us (5%)
  matrix products  2.43 us (3%)
    ppermute x4, starting transfers between devices, shifted(): return lax.ppermute(value, axis, pairs)  15.3 us
    ppermute x1, starting transfers between devices, shards(): lax.ppermute(five, 'ctx', [(s, s + 4) for s in range(ctx_count - 4)] + [(...  13.6 us
    ppermute x1, waiting for transfers between devices, shards(): tail = lax.ppermute(upto3, 'ctx', [(last, 0)])  10.7 us
    ppermute x1, waiting for transfers between devices, shards(): lax.ppermute(five, 'ctx', [(s, s + 4) for s in range(ctx_count - 4)] + [(...  8.27 us
    all_to_all x1, starting transfers between devices, shards(): square_total = jnp.sum(lax.all_to_all(part, ('chip', 'core'), 0, 0), axis=0)  6.54 us
    all_to_all x1, waiting for transfers between devices, shards(): square_total = jnp.sum(lax.all_to_all(part, ('chip', 'core'), 0, 0), axis=0)  4.41 us
    unnamed x14, local copies, waits for them, and re-layouts  2.72 us
    ppermute x4, waiting for transfers between devices, shifted(): return lax.ppermute(value, axis, pairs)  2.41 us
  transfers between devices with their start and end apart: 7, of which 4 were waited for; matrix products, arithmetic and copies ran while one was open for 3% of the time, Pallas kernels for 0%

profile of v10, /device:TPU:1, one launch (start us, length us, event | category | flops | bytes accessed | tf_op | source)
XLA Modules:
  0.0 73.8 jit_solution(16655060513815579773)
XLA Ops:
  0.0 0.0 copy-start
  0.1 0.0 copy-start.6
  0.1 0.7 copy-done.6
  0.8 0.0 copy-start.5
  0.8 0.7 copy-done.5
  1.4 0.3 reduce-window.9
  1.7 0.1 slice.23
  1.9 0.1 slice_reduce_fusion
  2.0 0.0 copy-start.2
  2.0 1.1 %copy.49 = bf16[256,512]{0,1:T(8,128)(2,1)S(1)} copy(bf16[256,512]{1,0:T(8,128)(2,1)} %param.9) | data formatting | bytes 524288 | tf_op jit(solution)/shard_map/reshape | solution.py:56
  3.1 0.0 copy-start.4
  3.2 0.7 copy-done.4
  3.8 0.1 select_reduce_fusion
  4.0 0.7 fusion.32
  4.7 0.2 convert_reduce_fusion
  4.8 0.2 convert_reduce_fusion.2
  5.1 0.1 exponential_select_fusion.3
  5.2 0.7 broadcast_compare_fusion.1
  5.9 0.1 exponential_select_fusion.2
  5.9 0.0 copy-done.1
  6.0 0.0 copy-done.2
  6.0 0.4 convolution_add_fusion
  6.4 4.4 %collective-permute-start.3 = (f32[4,128,128]{2,1,0:T(8,128)S(1)}, f32[4,128,128]{2,1,0:T(8,128)S(1)}, u32[]{:S(2)}, u32[]{:S(2)}) collective-permute-start(f32[4,128,128]{2,1,0:T(8,128)S(1)} %convolution_add_fusion), channel_id=1, source_target_pairs={{0,32},{8,40},{16,48},{24,56},{32,64},{40,72},{48,80},{56,88},{64,... | collective-permute-start | bytes 786440 | tf_op jit(solution)/shard_map/ppermute | solution.py:11
  10.8 4.7 %collective-permute-start.2 = (f32[4,128,128]{2,1,0:T(8,128)S(1)}, f32[4,128,128]{2,1,0:T(8,128)S(1)}, u32[]{:S(2)}, u32[]{:S(2)}) collective-permute-start(f32[4,128,128]{2,1,0:T(8,128)S(1)} %convolution_add_fusion), channel_id=1, source_target_pairs={{0,24},{8,32},{16,40},{24,48},{32,56},{40,64},{48,72},{56,80},{64,... | collective-permute-start | bytes 786440 | tf_op jit(solution)/shard_map/ppermute | solution.py:11
  15.4 3.6 %collective-permute-start.1 = (f32[4,128,128]{2,1,0:T(8,128)S(1)}, f32[4,128,128]{2,1,0:T(8,128)S(1)}, u32[]{:S(2)}, u32[]{:S(2)}) collective-permute-start(f32[4,128,128]{2,1,0:T(8,128)S(1)} %convolution_add_fusion), channel_id=1, source_target_pairs={{0,16},{8,24},{16,32},{24,40},{32,48},{40,56},{48,64},{56,72},{64,... | collective-permute-start | bytes 786440 | tf_op jit(solution)/shard_map/ppermute | solution.py:11
  19.0 2.6 %collective-permute-start = (f32[4,128,128]{2,1,0:T(8,128)S(1)}, f32[4,128,128]{2,1,0:T(8,128)S(1)}, u32[]{:S(2)}, u32[]{:S(2)}) collective-permute-start(f32[4,128,128]{2,1,0:T(8,128)S(1)} %convolution_add_fusion), channel_id=1, source_target_pairs={{0,8},{8,16},{16,24},{24,32},{32,40},{40,48},{48,56},{56,64},{64,7... | collective-permute-start | bytes 786440 | tf_op jit(solution)/shard_map/ppermute | solution.py:11
  21.7 0.1 fusion.7
  21.8 0.1 fusion.21
  21.9 0.0 copy-done
  21.9 0.4 fusion.4
  22.4 0.3 fusion
  22.7 0.0 collective-permute-done.3
  22.7 0.0 collective-permute-done.2
  22.7 0.0 collective-permute-done.1
  22.7 2.4 %collective-permute-done = f32[4,128,128]{2,1,0:T(8,128)S(1)} collective-permute-done((f32[4,128,128]{2,1,0:T(8,128)S(1)}, f32[4,128,128]{2,1,0:T(8,128)S(1)}, u32[]{:S(2)}, u32[]{:S(2)}) %collective-permute-start) | collective-permute-done | bytes 262176 | tf_op jit(solution)/shard_map/ppermute | solution.py:11
  25.1 0.1 multiply_add_fusion
  25.3 1.3 %collective-permute-start.5 = (f32[4,128,128]{2,1,0:T(8,128)S(1)}, f32[4,128,128]{2,1,0:T(8,128)S(1)}, u32[]{:S(2)}, u32[]{:S(2)}) collective-permute-start(f32[4,128,128]{2,1,0:T(8,128)S(1)} %get-tuple-element.10), channel_id=1, source_target_pairs={{1016,0},{1017,1},{1018,2},{1019,3},{1020,4},{1021,5},{1022,6},{10... | collective-permute-start | bytes 786440 | tf_op jit(solution)/shard_map/ppermute | solution.py:83
  26.6 13.6 %collective-permute-start.4 = (f32[4,128,128]{2,1,0:T(8,128)S(1)}, f32[4,128,128]{2,1,0:T(8,128)S(1)}, u32[]{:S(2)}, u32[]{:S(2)}) collective-permute-start(f32[4,128,128]{2,1,0:T(8,128)S(1)} %get-tuple-element.9), channel_id=1, source_target_pairs={{0,32},{8,40},{16,48},{24,56},{32,64},{40,72},{48,80},{56,88},{64,... | collective-permute-start | bytes 786440 | tf_op jit(solution)/shard_map/ppermute | solution.py:82
  40.2 0.7 convolution_bitcast_fusion.2
  40.9 10.7 %collective-permute-done.5 = f32[4,128,128]{2,1,0:T(8,128)S(1)} collective-permute-done((f32[4,128,128]{2,1,0:T(8,128)S(1)}, f32[4,128,128]{2,1,0:T(8,128)S(1)}, u32[]{:S(2)}, u32[]{:S(2)}) %collective-permute-start.5) | collective-permute-done | bytes 262176 | tf_op jit(solution)/shard_map/ppermute | solution.py:83
  51.7 8.3 %collective-permute-done.4 = f32[4,128,128]{2,1,0:T(8,128)S(1)} collective-permute-done((f32[4,128,128]{2,1,0:T(8,128)S(1)}, f32[4,128,128]{2,1,0:T(8,128)S(1)}, u32[]{:S(2)}, u32[]{:S(2)}) %collective-permute-start.4) | collective-permute-done | bytes 262176 | tf_op jit(solution)/shard_map/ppermute | solution.py:82
  59.9 0.6 multiply_reduce_fusion
  60.5 0.6 broadcast_in_dim.118
  61.1 6.5 %all-to-all-start = ((f32[8,1,256]{2,1,0:T(1,128)}), f32[8,1,256]{2,1,0:T(1,128)S(1)}, u32[]{:S(2)}, u32[]{:S(2)}) async-start(f32[8,1,256]{2,1,0:T(1,128)} %broadcast_in_dim.118), calls=%async_computation | async-start | bytes 16384 | tf_op jit(solution)/shard_map/all_to_all | solution.py:110
  67.6 0.2 copy.45
  67.8 4.4 %all-to-all-done = f32[8,1,256]{2,1,0:T(1,128)S(1)} async-done(((f32[8,1,256]{2,1,0:T(1,128)}), f32[8,1,256]{2,1,0:T(1,128)S(1)}, u32[]{:S(2)}, u32[]{:S(2)}) %all-to-all-start) | async-done | bytes 8224 | tf_op jit(solution)/shard_map/all_to_all | solution.py:110
  72.3 0.7 copy-done.3
  73.0 0.8 %multiply_convert_fusion = bf16[256,512]{1,0:T(8,128)(2,1)} fusion(f32[256,512]{1,0:T(8,128)S(1)} %copy.45, f32[512]{0:T(512)S(1)} %copy-done.3, f32[256]{0:T(256)S(1)} %add_rsqrt_fusion), kind=kLoop, calls=%fused_computation.10 | loop fusion | flops 393216 | bytes 789504 | tf_op jit(solution)/shard_map/convert_element_type | solution.py:112
  (13 shorter events, 0.1 us)
Async XLA Ops:
  0.0 21.9 %copy-start = (bf16[256,512]{1,0:T(8,128)(2,1)S(1)}, bf16[256,512]{1,0:T(8,128)(2,1)}, u32[]{:S(2)}) copy-start(bf16[256,512]{1,0:T(8,128)(2,1)} %param.8) | copy-start | bytes 786436
  0.1 0.7 copy-start.6
  0.8 0.7 copy-start.5
  2.0 4.0 %copy-start.1 = (bf16[256,512]{1,0:T(8,128)(2,1)S(1)}, bf16[256,512]{1,0:T(8,128)(2,1)}, u32[]{:S(2)}) copy-start(bf16[256,512]{1,0:T(8,128)(2,1)} %param.10) | copy-start | bytes 786436
  2.0 4.0 %copy-start.2 = (f32[4,128,128]{2,1,0:T(8,128)S(1)}, f32[4,128,128]{2,1,0:T(8,128)}, u32[]{:S(2)}) copy-start(f32[4,128,128]{2,1,0:T(8,128)} %param.11) | copy-start | bytes 786436
  3.1 0.7 copy-start.4
  6.4 16.3 %collective-permute-start.3 = (f32[4,128,128]{2,1,0:T(8,128)S(1)}, f32[4,128,128]{2,1,0:T(8,128)S(1)}, u32[]{:S(2)}, u32[]{:S(2)}) collective-permute-start(f32[4,128,128]{2,1,0:T(8,128)S(1)} %convolution_add_fusion), channel_id=1, source_target_pairs={{0,32},{8,40},{16,48},{24,56},{32,64},{40,72},{48,80},{56,88},{64,... | collective-permute-start | bytes 786440 | tf_op jit(solution)/shard_map/ppermute | solution.py:11
  10.8 12.0 %collective-permute-start.2 = (f32[4,128,128]{2,1,0:T(8,128)S(1)}, f32[4,128,128]{2,1,0:T(8,128)S(1)}, u32[]{:S(2)}, u32[]{:S(2)}) collective-permute-start(f32[4,128,128]{2,1,0:T(8,128)S(1)} %convolution_add_fusion), channel_id=1, source_target_pairs={{0,24},{8,32},{16,40},{24,48},{32,56},{40,64},{48,72},{56,80},{64,... | collective-permute-start | bytes 786440 | tf_op jit(solution)/shard_map/ppermute | solution.py:11
  15.4 7.3 %collective-permute-start.1 = (f32[4,128,128]{2,1,0:T(8,128)S(1)}, f32[4,128,128]{2,1,0:T(8,128)S(1)}, u32[]{:S(2)}, u32[]{:S(2)}) collective-permute-start(f32[4,128,128]{2,1,0:T(8,128)S(1)} %convolution_add_fusion), channel_id=1, source_target_pairs={{0,16},{8,24},{16,32},{24,40},{32,48},{40,56},{48,64},{56,72},{64,... | collective-permute-start | bytes 786440 | tf_op jit(solution)/shard_map/ppermute | solution.py:11
  19.0 6.1 %collective-permute-start = (f32[4,128,128]{2,1,0:T(8,128)S(1)}, f32[4,128,128]{2,1,0:T(8,128)S(1)}, u32[]{:S(2)}, u32[]{:S(2)}) collective-permute-start(f32[4,128,128]{2,1,0:T(8,128)S(1)} %convolution_add_fusion), channel_id=1, source_target_pairs={{0,8},{8,16},{16,24},{24,32},{32,40},{40,48},{48,56},{56,64},{64,7... | collective-permute-start | bytes 786440 | tf_op jit(solution)/shard_map/ppermute | solution.py:11
  25.3 26.4 %collective-permute-start.5 = (f32[4,128,128]{2,1,0:T(8,128)S(1)}, f32[4,128,128]{2,1,0:T(8,128)S(1)}, u32[]{:S(2)}, u32[]{:S(2)}) collective-permute-start(f32[4,128,128]{2,1,0:T(8,128)S(1)} %get-tuple-element.10), channel_id=1, source_target_pairs={{1016,0},{1017,1},{1018,2},{1019,3},{1020,4},{1021,5},{1022,6},{10... | collective-permute-start | bytes 786440 | tf_op jit(solution)/shard_map/ppermute | solution.py:83
  26.6 33.3 %collective-permute-start.4 = (f32[4,128,128]{2,1,0:T(8,128)S(1)}, f32[4,128,128]{2,1,0:T(8,128)S(1)}, u32[]{:S(2)}, u32[]{:S(2)}) collective-permute-start(f32[4,128,128]{2,1,0:T(8,128)S(1)} %get-tuple-element.9), channel_id=1, source_target_pairs={{0,32},{8,40},{16,48},{24,56},{32,64},{40,72},{48,80},{56,88},{64,... | collective-permute-start | bytes 786440 | tf_op jit(solution)/shard_map/ppermute | solution.py:82
  61.1 11.2 %all-to-all-start = ((f32[8,1,256]{2,1,0:T(1,128)}), f32[8,1,256]{2,1,0:T(1,128)S(1)}, u32[]{:S(2)}, u32[]{:S(2)}) async-start(f32[8,1,256]{2,1,0:T(1,128)} %broadcast_in_dim.118), calls=%async_computation | async-start | bytes 16384 | tf_op jit(solution)/shard_map/all_to_all | solution.py:110
  72.3 0.7 copy-start.3

commit v11 on v9

--- a/solution.py
+++ b/solution.py
@@ -91,6 +91,9 @@
     scores = jnp.einsum("thd,shd->hts", q, k, preferred_element_type=jnp.float32)
     weights = jnp.where(same_doc[None], scores * decay, jnp.float32(0.0))
     attn = jnp.einsum("hts,shd->thd", weights, v_f, precision=highest)
+    attn, gain_rows = lax.optimization_barrier(
+        (attn, jnp.broadcast_to(norm_gain[None, :], (row_count, feature_count)))
+    )
 
     lead_in = jnp.where(
         (segment == in_seg)[:, None],
@@ -111,7 +114,7 @@
     part = jnp.broadcast_to(jnp.sum(flat * flat, axis=1)[None], (groups, row_count))
     square_total = jnp.sum(lax.all_to_all(part, ("chip", "core"), 0, 0), axis=0)
     mean_sq = square_total / jnp.float32(feature_count * lax.axis_size("chip") * lax.axis_size("core"))
-    return (flat * lax.rsqrt(mean_sq + 1e-05)[:, None] * norm_gain[None, :]).astype(jnp.bfloat16)
+    return (flat * lax.rsqrt(mean_sq + 1e-05)[:, None] * gain_rows).astype(jnp.bfloat16)
 
 
 def solution(mesh):

time: 72.7 us -> 75 us (1.032)
  waiting for transfers between devices: 25.1 us -> 27.7 us
  other arithmetic: 3.71 us -> 2.95 us
    ppermute x1, waiting for transfers between devices: 0.01 us -> 10.3 us  [shards(): lax.ppermute(five, 'ctx', [(s, s + 4) for s in range(ctx_count - 4)] + [(...]
    ppermute x1, waiting for transfers between devices: 18.3 us -> 10.1 us  [shards(): tail = lax.ppermute(upto3, 'ctx', [(last - 5, 0)])]
    convert_element_type x0 -> x1, local copies, waits for them, and re-layouts: none -> 0.84 us  [shards(): (flat * lax.rsqrt(mean_sq + 1e-05)[:, None] * gain_rows).astype(jnp.bfloa...]
  transfers between devices with their start and end apart: 7 -> 7, of which waited for: 3 -> 4; matrix products, arithmetic and copies ran while one was open for 3% -> 3% of each run, Pallas kernels for 0% -> 0%
where the time goes in v11:
time: 75 us; the launch traced here: 74.7 us
  starting transfers between devices  36.2 us (48%)
  waiting for transfers between devices  27.7 us (37%)
  local copies, waits for them, and re-layouts  5.19 us (7%)
  other arithmetic  2.95 us (4%)
  matrix products  2.38 us (3%)
    ppermute x4, starting transfers between devices, shifted(): return lax.ppermute(value, axis, pairs)  15.3 us
    ppermute x1, starting transfers between devices, shards(): lax.ppermute(five, 'ctx', [(s, s + 4) for s in range(ctx_count - 4)] + [(...  14.2 us
    ppermute x1, waiting for transfers between devices, shards(): lax.ppermute(five, 'ctx', [(s, s + 4) for s in range(ctx_count - 4)] + [(...  10.3 us
    ppermute x1, waiting for transfers between devices, shards(): tail = lax.ppermute(upto3, 'ctx', [(last - 5, 0)])  10.1 us
    all_to_all x1, starting transfers between devices, shards(): square_total = jnp.sum(lax.all_to_all(part, ('chip', 'core'), 0, 0), axis=0)  5.44 us
    all_to_all x1, waiting for transfers between devices, shards(): square_total = jnp.sum(lax.all_to_all(part, ('chip', 'core'), 0, 0), axis=0)  4.41 us
    ppermute x4, waiting for transfers between devices, shifted(): return lax.ppermute(value, axis, pairs)  2.83 us
    unnamed x14, local copies, waits for them, and re-layouts  2.07 us
  transfers between devices with their start and end apart: 7, of which 4 were waited for; matrix products, arithmetic and copies ran while one was open for 3% of the time, Pallas kernels for 0%

profile of v11, /device:TPU:1, one launch (start us, length us, event | category | flops | bytes accessed | tf_op | source)
XLA Modules:
  0.0 74.7 jit_solution(15973788174020488760)
XLA Ops:
  0.0 0.0 copy-start
  0.1 0.0 copy-start.6
  0.1 0.7 copy-done.6
  0.8 0.7 copy-done.5
  1.4 0.3 reduce-window.9
  1.7 0.1 slice.29
  1.8 0.1 slice_reduce_fusion
  2.0 0.7 fusion.36
  2.7 0.2 convert_reduce_fusion.2
  2.9 0.1 exponential_select_fusion.3
  3.0 0.7 copy-done.4
  3.7 0.1 select_reduce_fusion
  3.8 0.2 convert_reduce_fusion
  4.0 0.0 copy-start.1
  4.0 0.0 copy-start.2
  4.0 1.1 %copy.61 = bf16[256,512]{0,1:T(8,128)(2,1)S(1)} copy(bf16[256,512]{1,0:T(8,128)(2,1)} %param.9) | data formatting | bytes 524288 | tf_op jit(solution)/shard_map/reshape | solution.py:56
  5.2 0.7 broadcast_compare_fusion.1
  5.8 0.1 exponential_select_fusion.2
  5.9 0.0 copy-done.1
  5.9 0.4 convolution_add_fusion
  6.3 4.4 %collective-permute-start.3 = (f32[4,128,128]{2,1,0:T(8,128)S(1)}, f32[4,128,128]{2,1,0:T(8,128)S(1)}, u32[]{:S(2)}, u32[]{:S(2)}) collective-permute-start(f32[4,128,128]{2,1,0:T(8,128)S(1)} %convolution_add_fusion), channel_id=1, source_target_pairs={{0,32},{8,40},{16,48},{24,56},{32,64},{40,72},{48,80},{56,88},{64,... | collective-permute-start | bytes 786440 | tf_op jit(solution)/shard_map/ppermute | solution.py:11
  10.7 4.7 %collective-permute-start.2 = (f32[4,128,128]{2,1,0:T(8,128)S(1)}, f32[4,128,128]{2,1,0:T(8,128)S(1)}, u32[]{:S(2)}, u32[]{:S(2)}) collective-permute-start(f32[4,128,128]{2,1,0:T(8,128)S(1)} %convolution_add_fusion), channel_id=1, source_target_pairs={{0,24},{8,32},{16,40},{24,48},{32,56},{40,64},{48,72},{56,80},{64,... | collective-permute-start | bytes 786440 | tf_op jit(solution)/shard_map/ppermute | solution.py:11
  15.4 3.6 %collective-permute-start.1 = (f32[4,128,128]{2,1,0:T(8,128)S(1)}, f32[4,128,128]{2,1,0:T(8,128)S(1)}, u32[]{:S(2)}, u32[]{:S(2)}) collective-permute-start(f32[4,128,128]{2,1,0:T(8,128)S(1)} %convolution_add_fusion), channel_id=1, source_target_pairs={{0,16},{8,24},{16,32},{24,40},{32,48},{40,56},{48,64},{56,72},{64,... | collective-permute-start | bytes 786440 | tf_op jit(solution)/shard_map/ppermute | solution.py:11
  19.0 2.6 %collective-permute-start = (f32[4,128,128]{2,1,0:T(8,128)S(1)}, f32[4,128,128]{2,1,0:T(8,128)S(1)}, u32[]{:S(2)}, u32[]{:S(2)}) collective-permute-start(f32[4,128,128]{2,1,0:T(8,128)S(1)} %convolution_add_fusion), channel_id=1, source_target_pairs={{0,8},{8,16},{16,24},{24,32},{32,40},{40,48},{48,56},{56,64},{64,7... | collective-permute-start | bytes 786440 | tf_op jit(solution)/shard_map/ppermute | solution.py:11
  21.6 0.1 fusion.24
  21.8 0.1 fusion.9
  21.9 0.3 fusion
  22.3 0.0 collective-permute-done.3
  22.3 0.0 collective-permute-done.2
  22.3 0.0 collective-permute-done.1
  22.3 2.8 %collective-permute-done = f32[4,128,128]{2,1,0:T(8,128)S(1)} collective-permute-done((f32[4,128,128]{2,1,0:T(8,128)S(1)}, f32[4,128,128]{2,1,0:T(8,128)S(1)}, u32[]{:S(2)}, u32[]{:S(2)}) %collective-permute-start) | collective-permute-done | bytes 262176 | tf_op jit(solution)/shard_map/ppermute | solution.py:11
  25.1 0.1 multiply_add_fusion
  25.3 14.2 %collective-permute-start.4 = (f32[4,128,128]{2,1,0:T(8,128)S(1)}, f32[4,128,128]{2,1,0:T(8,128)S(1)}, u32[]{:S(2)}, u32[]{:S(2)}) collective-permute-start(f32[4,128,128]{2,1,0:T(8,128)S(1)} %get-tuple-element.13), channel_id=1, source_target_pairs={{0,32},{8,40},{16,48},{24,56},{32,64},{40,72},{48,80},{56,88},{64,... | collective-permute-start | bytes 786440 | tf_op jit(solution)/shard_map/ppermute | solution.py:82
  39.5 0.0 copy-start.3
  39.5 1.3 %collective-permute-start.5 = (f32[4,128,128]{2,1,0:T(8,128)S(1)}, f32[4,128,128]{2,1,0:T(8,128)S(1)}, u32[]{:S(2)}, u32[]{:S(2)}) collective-permute-start(f32[4,128,128]{2,1,0:T(8,128)S(1)} %get-tuple-element.14), channel_id=1, source_target_pairs={{976,0},{977,1},{978,2},{979,3},{980,4},{981,5},{982,6},{983,7}} | collective-permute-start | bytes 786440 | tf_op jit(solution)/shard_map/ppermute | solution.py:83
  40.8 0.6 convolution_bitcast_fusion.2
  41.4 0.0 copy-done.3
  41.4 0.1 broadcast_in_dim.76
  41.6 0.4 fusion.4
  41.9 10.3 %collective-permute-done.4 = f32[4,128,128]{2,1,0:T(8,128)S(1)} collective-permute-done((f32[4,128,128]{2,1,0:T(8,128)S(1)}, f32[4,128,128]{2,1,0:T(8,128)S(1)}, u32[]{:S(2)}, u32[]{:S(2)}) %collective-permute-start.4) | collective-permute-done | bytes 262176 | tf_op jit(solution)/shard_map/ppermute | solution.py:82
  52.3 10.1 %collective-permute-done.5 = f32[4,128,128]{2,1,0:T(8,128)S(1)} collective-permute-done((f32[4,128,128]{2,1,0:T(8,128)S(1)}, f32[4,128,128]{2,1,0:T(8,128)S(1)}, u32[]{:S(2)}, u32[]{:S(2)}) %collective-permute-start.5) | collective-permute-done | bytes 262176 | tf_op jit(solution)/shard_map/ppermute | solution.py:83
  62.4 0.7 multiply_reduce_fusion
  63.0 0.6 broadcast_in_dim.124
  63.6 5.4 %all-to-all-start = ((f32[8,1,256]{2,1,0:T(1,128)}), f32[8,1,256]{2,1,0:T(1,128)S(1)}, u32[]{:S(2)}, u32[]{:S(2)}) async-start(f32[8,1,256]{2,1,0:T(1,128)} %broadcast_in_dim.124), calls=%async_computation | async-start | bytes 16384 | tf_op jit(solution)/shard_map/all_to_all | solution.py:115
  69.1 0.2 copy.53
  69.3 4.4 %all-to-all-done = f32[8,1,256]{2,1,0:T(1,128)S(1)} async-done(((f32[8,1,256]{2,1,0:T(1,128)}), f32[8,1,256]{2,1,0:T(1,128)S(1)}, u32[]{:S(2)}, u32[]{:S(2)}) %all-to-all-start) | async-done | bytes 8224 | tf_op jit(solution)/shard_map/all_to_all | solution.py:115
  73.7 0.1 fusion.6
  73.8 0.8 %copy.55 = bf16[256,512]{1,0:T(8,128)(2,1)} copy(bf16[256,512]{0,1:T(8,128)(2,1)S(1)} %fusion.6) | data formatting | bytes 524288 | tf_op jit(solution)/shard_map/convert_element_type | solution.py:117
  (16 shorter events, 0.2 us)
Async XLA Ops:
  0.0 21.9 %copy-start = (bf16[256,512]{1,0:T(8,128)(2,1)S(1)}, bf16[256,512]{1,0:T(8,128)(2,1)}, u32[]{:S(2)}) copy-start(bf16[256,512]{1,0:T(8,128)(2,1)} %param.8) | copy-start | bytes 786436
  0.1 0.7 copy-start.6
  0.7 0.7 copy-start.5
  3.0 0.7 copy-start.4
  4.0 1.9 %copy-start.1 = (bf16[256,512]{1,0:T(8,128)(2,1)S(1)}, bf16[256,512]{1,0:T(8,128)(2,1)}, u32[]{:S(2)}) copy-start(bf16[256,512]{1,0:T(8,128)(2,1)} %param.10) | copy-start | bytes 786436
  4.0 1.9 %copy-start.2 = (f32[4,128,128]{2,1,0:T(8,128)S(1)}, f32[4,128,128]{2,1,0:T(8,128)}, u32[]{:S(2)}) copy-start(f32[4,128,128]{2,1,0:T(8,128)} %param.11) | copy-start | bytes 786436
  6.3 15.9 %collective-permute-start.3 = (f32[4,128,128]{2,1,0:T(8,128)S(1)}, f32[4,128,128]{2,1,0:T(8,128)S(1)}, u32[]{:S(2)}, u32[]{:S(2)}) collective-permute-start(f32[4,128,128]{2,1,0:T(8,128)S(1)} %convolution_add_fusion), channel_id=1, source_target_pairs={{0,32},{8,40},{16,48},{24,56},{32,64},{40,72},{48,80},{56,88},{64,... | collective-permute-start | bytes 786440 | tf_op jit(solution)/shard_map/ppermute | solution.py:11
  10.7 11.5 %collective-permute-start.2 = (f32[4,128,128]{2,1,0:T(8,128)S(1)}, f32[4,128,128]{2,1,0:T(8,128)S(1)}, u32[]{:S(2)}, u32[]{:S(2)}) collective-permute-start(f32[4,128,128]{2,1,0:T(8,128)S(1)} %convolution_add_fusion), channel_id=1, source_target_pairs={{0,24},{8,32},{16,40},{24,48},{32,56},{40,64},{48,72},{56,80},{64,... | collective-permute-start | bytes 786440 | tf_op jit(solution)/shard_map/ppermute | solution.py:11
  15.4 6.9 %collective-permute-start.1 = (f32[4,128,128]{2,1,0:T(8,128)S(1)}, f32[4,128,128]{2,1,0:T(8,128)S(1)}, u32[]{:S(2)}, u32[]{:S(2)}) collective-permute-start(f32[4,128,128]{2,1,0:T(8,128)S(1)} %convolution_add_fusion), channel_id=1, source_target_pairs={{0,16},{8,24},{16,32},{24,40},{32,48},{40,56},{48,64},{56,72},{64,... | collective-permute-start | bytes 786440 | tf_op jit(solution)/shard_map/ppermute | solution.py:11
  19.0 6.1 %collective-permute-start = (f32[4,128,128]{2,1,0:T(8,128)S(1)}, f32[4,128,128]{2,1,0:T(8,128)S(1)}, u32[]{:S(2)}, u32[]{:S(2)}) collective-permute-start(f32[4,128,128]{2,1,0:T(8,128)S(1)} %convolution_add_fusion), channel_id=1, source_target_pairs={{0,8},{8,16},{16,24},{24,32},{32,40},{40,48},{48,56},{56,64},{64,7... | collective-permute-start | bytes 786440 | tf_op jit(solution)/shard_map/ppermute | solution.py:11
  25.3 27.0 %collective-permute-start.4 = (f32[4,128,128]{2,1,0:T(8,128)S(1)}, f32[4,128,128]{2,1,0:T(8,128)S(1)}, u32[]{:S(2)}, u32[]{:S(2)}) collective-permute-start(f32[4,128,128]{2,1,0:T(8,128)S(1)} %get-tuple-element.13), channel_id=1, source_target_pairs={{0,32},{8,40},{16,48},{24,56},{32,64},{40,72},{48,80},{56,88},{64,... | collective-permute-start | bytes 786440 | tf_op jit(solution)/shard_map/ppermute | solution.py:82
  39.5 1.9 %copy-start.3 = (f32[512]{0:T(512)S(1)}, f32[512]{0:T(512)}, u32[]{:S(2)}) copy-start(f32[512]{0:T(512)} %param.13) | copy-start | bytes 6148
  39.5 22.9 %collective-permute-start.5 = (f32[4,128,128]{2,1,0:T(8,128)S(1)}, f32[4,128,128]{2,1,0:T(8,128)S(1)}, u32[]{:S(2)}, u32[]{:S(2)}) collective-permute-start(f32[4,128,128]{2,1,0:T(8,128)S(1)} %get-tuple-element.14), channel_id=1, source_target_pairs={{976,0},{977,1},{978,2},{979,3},{980,4},{981,5},{982,6},{983,7}} | collective-permute-start | bytes 786440 | tf_op jit(solution)/shard_map/ppermute | solution.py:83
  63.6 10.1 %all-to-all-start = ((f32[8,1,256]{2,1,0:T(1,128)}), f32[8,1,256]{2,1,0:T(1,128)S(1)}, u32[]{:S(2)}, u32[]{:S(2)}) async-start(f32[8,1,256]{2,1,0:T(1,128)} %broadcast_in_dim.124), calls=%async_computation | async-start | bytes 16384 | tf_op jit(solution)/shard_map/all_to_all | solution.py:115
